TPU v7x, 512 devices: a whole 4x8x8 slice. The times are simulated.
512 devices in a mesh: req: 128 (over y, z, core), tp: 4 (over x).
Axes of the slice: x: 4, y: 8, z: 8, core: 2. Of those that a mesh axis runs over, the one named last changes fastest.
Arguments:
- tokens: bfloat16 [65536, 1024], P('req', 'tp')
- placement: int32 [16384], P('req'), may hold values from 0 to 16383, as said below
- cache_len: int32 [256], P('req'), may hold values from 0 to 1024, as said below
- w_query: bfloat16 [1024, 1024], P(None, 'tp'), may hold values from -0.1875 to 0.1875
- w_key: bfloat16 [1024, 1024], P(None, 'tp'), may hold values from -0.1875 to 0.1875
- w_value: bfloat16 [1024, 1024], P(None, 'tp'), may hold values from -0.1875 to 0.1875
- w_out: bfloat16 [1024, 1024], P('tp'), may hold values from -0.1875 to 0.1875
- k_cache: bfloat16 [256, 1024, 1024], P('req', None, 'tp'), may hold values from -6 to 6
- v_cache: bfloat16 [256, 1024, 1024], P('req', None, 'tp'), may hold values from -6 to 6
- ln_gain: float32 [1024], replicated, may hold values from 0.1 to 1.9
- ln_bias: float32 [1024], replicated, may hold values from -0.5 to 0.5
Outputs:
- mixed: bfloat16 [65536, 1024], P('req', 'tp')
Inputs may be any that keep to these rules, and one draw needn't show every extreme that they name: `placement`: A permutation of the blocks. Of the 128 blocks that arrive on index s of req, exactly one goes to the owner range of every index t of req, and it lands at owner position t * 128 + s. `cache_len`: some request has exactly 1024 cached positions.
All inputs are finite; a program needn't handle non-finite values.
Results may differ from a plain program's by a relative error of at most 0.014.
The roundings to bfloat16 on the way count: a program that leaves them out, or rounds other values in their place, can miss the bound.
Values may be sent and summed in bfloat16 or wider, within the bound.
No kernel may reach another device: no remote copies, remote signals or barrier semaphores. Data moves between devices by JAX's collectives and lax.ppermute only.
A program may use at most 64 MiB of HBM per device.

v0:
```python
import jax
import jax.numpy as jnp
from jax import lax
from jax.sharding import PartitionSpec as P

D = 1024
HEADS = 16


def head_view(array, head_size):
    return array.reshape(array.shape[0], array.shape[1] // head_size, head_size)


def attend_padded(queries, new_keys, new_values, cache_keys, cache_values, length):
    head_size = D // HEADS
    new_count = queries.shape[0]
    span = cache_keys.shape[0]
    keys_all = head_view(jnp.concatenate([cache_keys, new_keys], 0), head_size)
    values_all = head_view(jnp.concatenate([cache_values, new_values], 0), head_size)
    query_heads = head_view(queries, head_size)
    scores = jnp.einsum(
        "qhd,khd->hqk", query_heads, keys_all, preferred_element_type=jnp.float32
    ) * head_size ** (-0.5)
    key_pos = jnp.arange(span + new_count, dtype=jnp.int32)[None, :]
    query_pos = jnp.arange(new_count, dtype=jnp.int32)[:, None]
    valid = jnp.where(key_pos < span, key_pos < length, key_pos - span <= query_pos)
    scores = jnp.where(valid[None], scores, -jnp.inf)
    top = jnp.max(scores, axis=-1, keepdims=True)
    weight = jnp.where(valid[None], jnp.exp(scores - top), 0.0)
    total = jnp.sum(weight, axis=-1)
    context = jnp.einsum(
        "hqk,khd->qhd", weight.astype(jnp.bfloat16), values_all, preferred_element_type=jnp.float32
    )
    context = context / jnp.transpose(total)[:, :, None]
    return context.reshape(new_count, queries.shape[1]).astype(jnp.bfloat16)


def attend_all(queries, new_keys, new_values, k_cache, v_cache, cache_len):
    request_count = k_cache.shape[0]
    req_shape = (request_count, queries.shape[0] // request_count, queries.shape[1])
    context = lax.map(
        lambda items: attend_padded(*items),
        (
            queries.reshape(req_shape),
            new_keys.reshape(req_shape),
            new_values.reshape(req_shape),
            k_cache,
            v_cache,
            cache_len,
        ),
    )
    return context.reshape(queries.shape)


def project_rows(whole, w_query, w_key, w_value):
    queries = jnp.dot(whole, w_query, preferred_element_type=jnp.float32).astype(jnp.bfloat16)
    new_keys = jnp.dot(whole, w_key, preferred_element_type=jnp.float32).astype(jnp.bfloat16)
    new_values = jnp.dot(whole, w_value, preferred_element_type=jnp.float32).astype(jnp.bfloat16)
    return (queries, new_keys, new_values)


def finish_rows(context, local, w_out, ln_gain, ln_bias):
    row_count, feat_width = local.shape
    partial_sum = jnp.dot(context, w_out, preferred_element_type=jnp.float32)
    attended = lax.psum_scatter(
        partial_sum.astype(jnp.bfloat16), "tp", scatter_dimension=1, tiled=True
    ).astype(jnp.float32)
    summed = local.astype(jnp.float32) + attended
    first_sum, square_sum = lax.psum(
        (jnp.sum(summed, axis=1), jnp.sum(summed * summed, axis=1)), "tp"
    )
    row_mean = first_sum / D
    row_var = square_sum / D - row_mean * row_mean
    offset = lax.axis_index("tp") * feat_width
    gain_part = lax.dynamic_slice_in_dim(ln_gain, offset, feat_width, 0)
    bias_part = lax.dynamic_slice_in_dim(ln_bias, offset, feat_width, 0)
    scaled = (summed - row_mean[:, None]) / jnp.sqrt(row_var[:, None] + 1e-05)
    return (scaled * gain_part + bias_part).astype(jnp.bfloat16)


def shards(
    tokens, placement, cache_len, w_query, w_key, w_value, w_out, k_cache, v_cache, ln_gain, ln_bias
):
    row_count, feat_width = tokens.shape
    block_count = placement.shape[0]
    block_rows = row_count // block_count
    per_peer = block_count // lax.axis_size("req")
    send_slot = placement // block_count * per_peer + placement % per_peer
    send_order = (
        jnp.zeros((block_count,), jnp.int32)
        .at[send_slot]
        .set(jnp.arange(block_count, dtype=jnp.int32))
    )

    def to_blocks(array):
        return array.reshape(block_count, block_rows, array.shape[1])

    arrived = lax.all_to_all(
        to_blocks(tokens)[send_order], "req", split_axis=0, concat_axis=0, tiled=True
    ).reshape(row_count, feat_width)
    whole = lax.all_gather(arrived, "tp", axis=1, tiled=True)
    queries, new_keys, new_values = project_rows(whole, w_query, w_key, w_value)
    context = attend_all(queries, new_keys, new_values, k_cache, v_cache, cache_len)
    normed = finish_rows(context, arrived, w_out, ln_gain, ln_bias)
    returned = lax.all_to_all(to_blocks(normed), "req", split_axis=0, concat_axis=0, tiled=True)
    return returned[send_slot].reshape(row_count, feat_width)


def solution(mesh):
    in_specs = (
        P("req", "tp"),
        P("req"),
        P("req"),
        P(None, "tp"),
        P(None, "tp"),
        P(None, "tp"),
        P("tp", None),
        P("req", None, "tp"),
        P("req", None, "tp"),
        P(),
        P(),
    )
    out_specs = P("req", "tp")
    return jax.shard_map(shards, mesh=mesh, in_specs=in_specs, out_specs=out_specs, check_vma=False)
```

profile of v0, /device:TPU:1, one launch (start us, length us, event | category | flops | bytes accessed | tf_op | source)
XLA Modules:
  0.0 176.8 jit_solution(9790313830979759242)
XLA Ops:
  7.3 1.0 scatter_custom_fusion
  8.3 1.0 reshape.143
  10.1 32.5 %all_to_all.10 = bf16[128,4,256]{2,1,0:T(4,128)(2,1)S(1)} all-to-all(bf16[128,4,256]{2,1,0:T(4,128)(2,1)S(1)} %gather_fusion), channel_id=1, replica_groups=mesh['req'=128,'tp'=4] {'req'}, dimensions={0} | all-to-all | bytes 524288 | tf_op jit(solution)/shard_map/all_to_all | solution.py:98
  43.5 22.3 %all-gather.2.cloned.1.call-done = bf16[512,1024]{1,0:T(8,128)(2,1)} async-done(((bf16[512,256]{1,0:T(8,128)(2,1)}), bf16[512,1024]{1,0:T(8,128)(2,1)}) %all-gather.2.cloned.1.call-update) | async-done | bytes 1048592 | tf_op jit(solution)/shard_map/all_gather | solution.py:101
  65.8 2.5 %convolution_convert_fusion.2 = bf16[512,256]{1,0:T(8,128)(2,1)} fusion(bf16[512,1024]{1,0:T(8,128)(2,1)} %all-gather.2.cloned.1.call-done, bf16[1024,256]{1,0:T(8,128)(2,1)S(1)} %copy-done.8), kind=kOutput, calls=%fused_computation.43 | convolution fusion | flops 268566528 | bytes 1835008 | tf_op jit(solution)/shard_map/dot_general | solution.py:56
  68.3 1.1 convolution_convert_fusion.1
  69.4 1.1 convolution_convert_fusion.3
  70.7 23.4 %while.12 = (s32[]{:T(128)}, bf16[2,256,256]{2,1,0:T(8,128)(2,1)}, bf16[2,1024,256]{2,1,0:T(8,128)(2,1)S(1)}, bf16[2,256,256]{2,1,0:T(8,128)(2,1)}, s32[2]{0:T(1...) while((s32[]{:T(128)}, bf16[2,256,256]{2,1,0:T(8,128)(2,1)}, ...), condition=%wide.region_4.5_spmd, body=%wide.region_1.4_spmd.sunk | while | flops 521149696 | bytes 12803309 | solution.py:41
  72.2 1.1 constant_dynamic-slice_fusion.9
  73.6 1.0 constant_dynamic-slice_fusion.10
  74.8 2.3 %fusion.77 = f32[4,256]{1,0:T(4,128)S(1)} fusion(pred[256,1280]{1,0:T(8,128)(4,1)S(1)} %fusion.76, bf16[256,4,64]{0,2,1:T(8,128)(2,1)S(1)} %bitcast.53, bf16[256,4,64]{0,2,1:T(8,128)(2,1)S(1)} %bitcast.55, bf16[1024,4,64]{0,2,1:T(8,128)(2,1)S(1)} %bitcast.50), kind=kOutput, calls=%fused_computation.7.clone.1 | convolution fusion | flops 175637760 | bytes 1118208 | tf_op jit(solution)/shard_map/while/body/eval_jaxpr/sub | solution.py:29
  77.4 0.9 constant_dynamic-slice_fusion.8
  78.4 3.1 %fusion.78 = bf16[256,4,64]{0,2,1:T(8,128)(2,1)S(1)} fusion(pred[256,1280]{1,0:T(8,128)(4,1)S(1)} %fusion.76, bf16[256,4,64]{0,2,1:T(8,128)(2,1)S(1)} %bitcast.57, bf16[1024,4,64]{0,2,1:T(8,128)(2,1)S(1)} %bitcast.52, bf16[256,4,64]{0,2,1:T(8,128)(2,1)} %bitcast.54, bf16[256,4,64]{0,2,1:T(8,128)(2,1)} %bitcast.56, ...), kind=kOutput, calls=%fused_computation.16.clone.1 | convolution fusion | flops 344852736 | bytes 1904640 | tf_op jit(solution)/shard_map/while/body/eval_jaxpr/hqk,khd->qhd/dot_general | solution.py:31
  84.0 1.1 constant_dynamic-slice_fusion.9
  85.3 1.0 constant_dynamic-slice_fusion.10
  86.5 2.3 %fusion.77 = f32[4,256]{1,0:T(4,128)S(1)} fusion(pred[256,1280]{1,0:T(8,128)(4,1)S(1)} %fusion.76, bf16[256,4,64]{0,2,1:T(8,128)(2,1)S(1)} %bitcast.53, bf16[256,4,64]{0,2,1:T(8,128)(2,1)S(1)} %bitcast.55, bf16[1024,4,64]{0,2,1:T(8,128)(2,1)S(1)} %bitcast.50), kind=kOutput, calls=%fused_computation.7.clone.1 | convolution fusion | flops 175637760 | bytes 1118208 | tf_op jit(solution)/shard_map/while/body/eval_jaxpr/sub | solution.py:29
  90.1 3.1 %fusion.78 = bf16[256,4,64]{0,2,1:T(8,128)(2,1)S(1)} fusion(pred[256,1280]{1,0:T(8,128)(4,1)S(1)} %fusion.76, bf16[256,4,64]{0,2,1:T(8,128)(2,1)S(1)} %bitcast.57, bf16[1024,4,64]{0,2,1:T(8,128)(2,1)S(1)} %bitcast.52, bf16[256,4,64]{0,2,1:T(8,128)(2,1)} %bitcast.54, bf16[256,4,64]{0,2,1:T(8,128)(2,1)} %bitcast.56, ...), kind=kOutput, calls=%fused_computation.16.clone.1 | convolution fusion | flops 344852736 | bytes 1904640 | tf_op jit(solution)/shard_map/while/body/eval_jaxpr/hqk,khd->qhd/dot_general | solution.py:31
  94.1 2.4 %convolution_convert_fusion = bf16[512,1024]{1,0:T(8,128)(2,1)} fusion(bf16[512,256]{1,0:T(8,128)(2,1)} %bitcast.62, bf16[256,1024]{1,0:T(8,128)(2,1)S(1)} %copy-done), kind=kOutput, calls=%fused_computation.41 | convolution fusion | flops 268959744 | bytes 1835008 | tf_op jit(solution)/shard_map/dot_general | solution.py:64
  98.1 28.8 %reduce-scatter.2.cloned.1.call-done = bf16[512,256]{1,0:T(8,128)(2,1)} async-done(((bf16[512,1024]{1,0:T(8,128)(2,1)}), bf16[512,256]{1,0:T(8,128)(2,1)}) %reduce-scatter.2.cloned.1.call-update) | async-done | bytes 262160 | tf_op jit(solution)/shard_map/reduce_scatter | solution.py:65
  126.9 1.2 fusion.46
  128.1 6.7 %all-reduce = (f32[512]{0:T(512)S(1)}, f32[512]{0:T(512)S(1)}) all-reduce(f32[512]{0:T(512)S(1)} %get-tuple-element.124, f32[512]{0:T(512)S(1)} %get-tuple-element.123), channel_id=1, replica_groups=mesh['req'=128,'tp'=4] {'tp'}, use_global_device_ids=true, to_apply=%region_9.10 | all-reduce | flops 1024 | bytes 8192 | tf_op jit(solution)/shard_map/psum | solution.py:69
  134.7 1.2 add_convert_fusion
  136.7 17.4 %all-to-all-start.1 = ((bf16[128,4,256]{2,1,0:T(4,128)(2,1)}), bf16[128,4,256]{2,1,0:T(4,128)(2,1)S(1)}, u32[]{:S(2)}, u32[]{:S(2)}) async-start(bf16[128,4,256]{2,1,0:T(4,128)(2,1)} %reshape.149), calls=%async_computation.2 | async-start | bytes 524288 | tf_op jit(solution)/shard_map/all_to_all | solution.py:105
  154.1 14.2 %all-to-all-done.1 = bf16[128,4,256]{2,1,0:T(4,128)(2,1)S(1)} async-done(((bf16[128,4,256]{2,1,0:T(4,128)(2,1)}), bf16[128,4,256]{2,1,0:T(4,128)(2,1)S(1)}, u32[]{:S(2)}, u32[]{:S(2)}) %all-to-all-start.1) | async-done | bytes 262176 | tf_op jit(solution)/shard_map/all_to_all | solution.py:105
  (73 shorter events, 13.5 us)
Async XLA Ops:
  6.5 87.6 %copy-start = (bf16[256,1024]{1,0:T(8,128)(2,1)S(1)}, bf16[256,1024]{1,0:T(8,128)(2,1)}, u32[]{:S(2)}) copy-start(bf16[256,1024]{1,0:T(8,128)(2,1)} %param.19) | copy-start | bytes 1572868
  6.5 59.3 %all-gather.2.cloned.1.call-start = ((), (), s32[]{:S(2)}) async-start(), calls=%async_computation.3 | async-start | bytes 1310720 | tf_op jit(solution)/shard_map/all_gather | solution.py:101
  9.3 56.5 %copy-start.8 = (bf16[1024,256]{1,0:T(8,128)(2,1)S(1)}, bf16[1024,256]{1,0:T(8,128)(2,1)}, u32[]{:S(2)}) copy-start(bf16[1024,256]{1,0:T(8,128)(2,1)} %param.16) | copy-start | bytes 1572868
  43.4 24.9 %copy-start.9 = (bf16[1024,256]{1,0:T(8,128)(2,1)S(1)}, bf16[1024,256]{1,0:T(8,128)(2,1)}, u32[]{:S(2)}) copy-start(bf16[1024,256]{1,0:T(8,128)(2,1)} %param.17) | copy-start | bytes 1572868
  43.5 83.4 %reduce-scatter.2.cloned.1.call-start = ((), (), s32[]{:S(2)}) async-start(), calls=%async_computation.4 | async-start | bytes 1310720 | tf_op jit(solution)/shard_map/reduce_scatter | solution.py:65
  65.8 2.5 %copy-start.7 = (bf16[512,1024]{1,0:T(8,128)(2,1)S(1)}, bf16[512,1024]{1,0:T(8,128)(2,1)}, u32[]{:S(2)}) copy-start(bf16[512,1024]{1,0:T(8,128)(2,1)} %all-gather.2.cloned.1.call-done) | copy-start | bytes 3145732
  68.3 1.1 copy-start.10
  69.4 1.2 copy-start.1
  69.4 1.2 copy-start.11
  74.7 2.5 %copy-start.3 = (bf16[1,256,256]{1,2,0:T(8,128)(2,1)}, bf16[1,256,256]{1,2,0:T(8,128)(2,1)S(1)}, u32[]{:S(2)}) copy-start(bf16[1,256,256]{1,2,0:T(8,128)(2,1)S(1)} %copy.38) | copy-start | bytes 393220 | tf_op jit(solution)/shard_map/while
  74.8 2.3 %copy-start.4 = (bf16[1,256,256]{1,2,0:T(8,128)(2,1)}, bf16[1,256,256]{1,2,0:T(8,128)(2,1)S(1)}, u32[]{:S(2)}) copy-start(bf16[1,256,256]{1,2,0:T(8,128)(2,1)S(1)} %copy.39) | copy-start | bytes 393220 | tf_op jit(solution)/shard_map/while
  78.4 3.3 %copy-start.5 = (bf16[2,256,256]{2,1,0:T(8,128)(2,1)S(1)}, bf16[2,256,256]{2,1,0:T(8,128)(2,1)}, u32[]{:S(2)}) copy-start(bf16[2,256,256]{2,1,0:T(8,128)(2,1)} %get-tuple-element.222) | copy-start | bytes 786436 | tf_op jit(solution)/shard_map/while
  81.7 0.7 copy-start.6
  86.4 2.5 %copy-start.3 = (bf16[1,256,256]{1,2,0:T(8,128)(2,1)}, bf16[1,256,256]{1,2,0:T(8,128)(2,1)S(1)}, u32[]{:S(2)}) copy-start(bf16[1,256,256]{1,2,0:T(8,128)(2,1)S(1)} %copy.38) | copy-start | bytes 393220 | tf_op jit(solution)/shard_map/while
  86.5 2.3 %copy-start.4 = (bf16[1,256,256]{1,2,0:T(8,128)(2,1)}, bf16[1,256,256]{1,2,0:T(8,128)(2,1)S(1)}, u32[]{:S(2)}) copy-start(bf16[1,256,256]{1,2,0:T(8,128)(2,1)S(1)} %copy.39) | copy-start | bytes 393220 | tf_op jit(solution)/shard_map/while
  90.1 3.3 %copy-start.5 = (bf16[2,256,256]{2,1,0:T(8,128)(2,1)S(1)}, bf16[2,256,256]{2,1,0:T(8,128)(2,1)}, u32[]{:S(2)}) copy-start(bf16[2,256,256]{2,1,0:T(8,128)(2,1)} %get-tuple-element.222) | copy-start | bytes 786436 | tf_op jit(solution)/shard_map/while
  93.4 0.7 copy-start.6
  94.1 32.8 %copy-start.2 = (bf16[512,256]{1,0:T(8,128)(2,1)S(1)}, bf16[512,256]{1,0:T(8,128)(2,1)}, u32[]{:S(2)}) copy-start(bf16[512,256]{1,0:T(8,128)(2,1)} %reshape.144) | copy-start | bytes 786436
  136.7 31.7 %all-to-all-start.1 = ((bf16[128,4,256]{2,1,0:T(4,128)(2,1)}), bf16[128,4,256]{2,1,0:T(4,128)(2,1)S(1)}, u32[]{:S(2)}, u32[]{:S(2)}) async-start(bf16[128,4,256]{2,1,0:T(4,128)(2,1)} %reshape.149), calls=%async_computation.2 | async-start | bytes 524288 | tf_op jit(solution)/shard_map/all_to_all | solution.py:105
Sparse Core Ops, SparseCore 0:
  43.6 22.1 all-gather.1
  96.6 30.1 reduce-scatter.1
where the time goes:
time: 178 us; the launch traced here: 177 us
  waiting for transfers between devices  65.4 us (37%)
  blocking collectives  39.2 us (22%)
  matrix products  18.1 us (10%)
  local copies, waits for them, and re-layouts  18 us (10%)
  starting transfers between devices  17.5 us (10%)
  between operations  13.5 us (8%)
  other arithmetic  4.9 us (3%)
    all_to_all x1, blocking collectives, shards(): lax.all_to_all(to_blocks(tokens)[send_order], 'req', split_axis=0, concat...  32.5 us
    reduce_scatter x1, waiting for transfers between devices, finish_rows(): lax.psum_scatter(partial_sum.astype(jnp.bfloat16), 'tp', scatter_dimensio...  28.8 us
    all_gather x1, waiting for transfers between devices, shards(): whole = lax.all_gather(arrived, 'tp', axis=1, tiled=True)  22.3 us
    all_to_all x1, starting transfers between devices, shards(): lax.all_to_all(to_blocks(normed), 'req', split_axis=0, concat_axis=0, til...  17.4 us
    all_to_all x1, waiting for transfers between devices, shards(): lax.all_to_all(to_blocks(normed), 'req', split_axis=0, concat_axis=0, til...  14.2 us
    dynamic_slice x18, local copies, waits for them, and re-layouts, attend_all(): lax.map(lambda items: attend_padded(*items), (queries.reshape(req_shape),...  8.77 us
    psum x1, blocking collectives, finish_rows(): lax.psum((jnp.sum(summed, axis=1), jnp.sum(summed * summed, axis=1)), 'tp')  6.66 us
    dot_general x2, matrix products, attend_padded(): jnp.einsum('hqk,khd->qhd', weight.astype(jnp.bfloat16), values_all, prefe...  6.26 us
  transfers between devices with their start and end apart: 3, of which 3 were waited for; matrix products, arithmetic and copies ran while one was open for 1% of the time, Pallas kernels for 0%

commit v1 on v0

--- a/solution.py
+++ b/solution.py
@@ -5,6 +5,28 @@
 
 D = 1024
 HEADS = 16
+
+
+def gather_tp(part):
+    count = lax.axis_size("tp")
+    copies = jnp.broadcast_to(part[None], (count,) + part.shape)
+    got = lax.all_to_all(copies, "tp", 0, 0, tiled=True)
+    return jnp.moveaxis(got, 0, 1).reshape(part.shape[0], count * part.shape[1])
+
+
+def scatter_sum_tp(whole):
+    count = lax.axis_size("tp")
+    rows, width = whole.shape
+    pieces = jnp.moveaxis(whole.reshape(rows, count, width // count), 1, 0)
+    got = lax.all_to_all(pieces, "tp", 0, 0, tiled=True)
+    return jnp.sum(got.astype(jnp.float32), axis=0)
+
+
+def sum_tp(stats):
+    count = lax.axis_size("tp")
+    copies = jnp.broadcast_to(stats[None], (count,) + stats.shape)
+    got = lax.all_to_all(copies, "tp", 0, 0, tiled=True)
+    return jnp.sum(got, axis=0)
 
 
 def head_view(array, head_size):
@@ -62,12 +84,10 @@
 def finish_rows(context, local, w_out, ln_gain, ln_bias):
     row_count, feat_width = local.shape
     partial_sum = jnp.dot(context, w_out, preferred_element_type=jnp.float32)
-    attended = lax.psum_scatter(
-        partial_sum.astype(jnp.bfloat16), "tp", scatter_dimension=1, tiled=True
-    ).astype(jnp.float32)
+    attended = scatter_sum_tp(partial_sum.astype(jnp.bfloat16))
     summed = local.astype(jnp.float32) + attended
-    first_sum, square_sum = lax.psum(
-        (jnp.sum(summed, axis=1), jnp.sum(summed * summed, axis=1)), "tp"
+    first_sum, square_sum = sum_tp(
+        jnp.stack([jnp.sum(summed, axis=1), jnp.sum(summed * summed, axis=1)])
     )
     row_mean = first_sum / D
     row_var = square_sum / D - row_mean * row_mean
@@ -98,7 +118,7 @@
     arrived = lax.all_to_all(
         to_blocks(tokens)[send_order], "req", split_axis=0, concat_axis=0, tiled=True
     ).reshape(row_count, feat_width)
-    whole = lax.all_gather(arrived, "tp", axis=1, tiled=True)
+    whole = gather_tp(arrived)
     queries, new_keys, new_values = project_rows(whole, w_query, w_key, w_value)
     context = attend_all(queries, new_keys, new_values, k_cache, v_cache, cache_len)
     normed = finish_rows(context, arrived, w_out, ln_gain, ln_bias)

time: 178 us -> 137 us (0.77)
  waiting for transfers between devices: 65.4 us -> 29.9 us
  between operations: 13.5 us -> 0.16 us
  blocking collectives: 39.2 us -> 47 us
  matrix products: 18.1 us -> 15.9 us
  starting transfers between devices: 17.5 us -> 19.5 us
    reduce_scatter x1 -> x0, waiting for transfers between devices: 28.8 us -> none  [finish_rows(): lax.psum_scatter(partial_sum.astype(jnp.bfloat16), 'tp', scatter_dimensio...]
    all_gather x1 -> x0, waiting for transfers between devices: 22.3 us -> none  [shards(): whole = lax.all_gather(arrived, 'tp', axis=1, tiled=True)]
    all_to_all x0 -> x2, waiting for transfers between devices: none -> 15.7 us  [the longest x1 13.2 us: gather_tp(): got = lax.all_to_all(copies, 'tp', 0, 0, tiled=True)]
    all_to_all x0 -> x1, blocking collectives: none -> 14.5 us  [scatter_sum_tp(): got = lax.all_to_all(pieces, 'tp', 0, 0, tiled=True)]
    all_to_all x0 -> x2, starting transfers between devices: none -> 7.58 us  [the longest x1 4.14 us: gather_tp(): got = lax.all_to_all(copies, 'tp', 0, 0, tiled=True)]
    psum x1 -> x0, blocking collectives: 6.66 us -> none  [finish_rows(): lax.psum((jnp.sum(summed, axis=1), jnp.sum(summed * summed, axis=1)), 'tp')]
    all_to_all x1, starting transfers between devices: 17.4 us -> 11.9 us  [shards(): lax.all_to_all(to_blocks(normed), 'req', split_axis=0, concat_axis=0, til...]
    broadcast_in_dim x0 -> x4, local copies, waits for them, and re-layouts: none -> 1.89 us  [the longest x3 1.28 us: gather_tp(): copies = jnp.broadcast_to(part[None], (count,) + part.shape)]
where the time goes in v1:
time: 137 us; the launch traced here: 136 us
  blocking collectives  47 us (34%)
  waiting for transfers between devices  29.9 us (22%)
  local copies, waits for them, and re-layouts  19.6 us (14%)
  starting transfers between devices  19.5 us (14%)
  matrix products  15.9 us (12%)
  other arithmetic  4.15 us (3%)
    all_to_all x1, blocking collectives, shards(): lax.all_to_all(to_blocks(tokens)[send_order], 'req', split_axis=0, concat...  32.5 us
    all_to_all x1, blocking collectives, scatter_sum_tp(): got = lax.all_to_all(pieces, 'tp', 0, 0, tiled=True)  14.5 us
    all_to_all x1, waiting for transfers between devices, shards(): lax.all_to_all(to_blocks(normed), 'req', split_axis=0, concat_axis=0, til...  14.2 us
    all_to_all x1, waiting for transfers between devices, gather_tp(): got = lax.all_to_all(copies, 'tp', 0, 0, tiled=True)  13.2 us
    all_to_all x1, starting transfers between devices, shards(): lax.all_to_all(to_blocks(normed), 'req', split_axis=0, concat_axis=0, til...  11.9 us
    dynamic_slice x18, local copies, waits for them, and re-layouts, attend_all(): lax.map(lambda items: attend_padded(*items), (queries.reshape(req_shape),...  8.77 us
    dot_general x2, matrix products, attend_padded(): jnp.einsum('hqk,khd->qhd', weight.astype(jnp.bfloat16), values_all, prefe...  6.26 us
    sub x2, matrix products, attend_padded(): weight = jnp.where(valid[None], jnp.exp(scores - top), 0.0)  4.66 us
  transfers between devices with their start and end apart: 3, of which 3 were waited for; matrix products, arithmetic and copies ran while one was open for 1% of the time, Pallas kernels for 0%

profile of v1, /device:TPU:1, one launch (start us, length us, event | category | flops | bytes accessed | tf_op | source)
XLA Modules:
  0.0 136.5 jit_solution(8985920144651857273)
XLA Ops:
  1.7 1.0 reshape.193
  3.6 32.5 %all_to_all.25 = bf16[128,4,256]{2,1,0:T(4,128)(2,1)S(1)} all-to-all(bf16[128,4,256]{2,1,0:T(4,128)(2,1)S(1)} %gather_fusion), channel_id=1, replica_groups=mesh['req'=128,'tp'=4] {'req'}, dimensions={0} | all-to-all | bytes 524288 | tf_op jit(solution)/shard_map/all_to_all | solution.py:118
  36.3 1.1 broadcast_in_dim.83
  37.4 4.1 %all-to-all-start.1 = ((bf16[4,512,256]{1,2,0:T(8,128)(2,1)}), bf16[4,512,256]{1,2,0:T(8,128)(2,1)S(1)}, u32[]{:S(2)}, u32[]{:S(2)}) async-start(bf16[4,512,256]{1,2,0:T(8,128)(2,1)} %broadcast_in_dim.83), calls=%async_computation.1 | async-start | bytes 2097152 | tf_op jit(solution)/shard_map/all_to_all | solution.py:13
  41.6 13.2 %all-to-all-done.1 = bf16[4,512,256]{1,2,0:T(8,128)(2,1)S(1)} async-done(((bf16[4,512,256]{1,2,0:T(8,128)(2,1)}), bf16[4,512,256]{1,2,0:T(8,128)(2,1)S(1)}, u32[]{:S(2)}, u32[]{:S(2)}) %all-to-all-start.1) | async-done | bytes 1048608 | tf_op jit(solution)/shard_map/all_to_all | solution.py:13
  54.8 1.2 convolution_convert_fusion.3
  56.0 1.2 convolution_convert_fusion.2
  57.2 1.2 convolution_convert_fusion.1
  58.4 23.3 %while.12 = (s32[]{:T(128)}, bf16[2,256,256]{2,1,0:T(8,128)(2,1)}, bf16[2,1024,256]{2,1,0:T(8,128)(2,1)S(1)}, bf16[2,256,256]{2,1,0:T(8,128)(2,1)}, s32[2]{0:T(1...) while((s32[]{:T(128)}, bf16[2,256,256]{2,1,0:T(8,128)(2,1)}, ...), condition=%wide.region_4.5_spmd, body=%wide.region_1.4_spmd.sunk | while | flops 521149696 | bytes 12803309 | solution.py:63
  59.9 1.1 constant_dynamic-slice_fusion.9
  61.3 1.0 constant_dynamic-slice_fusion.10
  62.5 2.3 %fusion.79 = f32[4,256]{1,0:T(4,128)S(1)} fusion(pred[256,1280]{1,0:T(8,128)(4,1)S(1)} %fusion.78, bf16[256,4,64]{0,2,1:T(8,128)(2,1)S(1)} %bitcast.65, bf16[256,4,64]{0,2,1:T(8,128)(2,1)S(1)} %bitcast.67, bf16[1024,4,64]{0,2,1:T(8,128)(2,1)S(1)} %bitcast.60), kind=kOutput, calls=%fused_computation.7.clone.1 | convolution fusion | flops 175637760 | bytes 1118208 | tf_op jit(solution)/shard_map/while/body/eval_jaxpr/sub | solution.py:51
  66.1 3.1 %fusion.80 = bf16[256,4,64]{0,2,1:T(8,128)(2,1)S(1)} fusion(pred[256,1280]{1,0:T(8,128)(4,1)S(1)} %fusion.78, bf16[256,4,64]{0,2,1:T(8,128)(2,1)S(1)} %bitcast.69, bf16[1024,4,64]{0,2,1:T(8,128)(2,1)S(1)} %bitcast.62, bf16[256,4,64]{0,2,1:T(8,128)(2,1)} %bitcast.66, bf16[256,4,64]{0,2,1:T(8,128)(2,1)} %bitcast.68, ...), kind=kOutput, calls=%fused_computation.16.clone.1 | convolution fusion | flops 344852736 | bytes 1904640 | tf_op jit(solution)/shard_map/while/body/eval_jaxpr/hqk,khd->qhd/dot_general | solution.py:53
  71.6 1.1 constant_dynamic-slice_fusion.9
  72.9 1.0 constant_dynamic-slice_fusion.10
  74.2 2.3 %fusion.79 = f32[4,256]{1,0:T(4,128)S(1)} fusion(pred[256,1280]{1,0:T(8,128)(4,1)S(1)} %fusion.78, bf16[256,4,64]{0,2,1:T(8,128)(2,1)S(1)} %bitcast.65, bf16[256,4,64]{0,2,1:T(8,128)(2,1)S(1)} %bitcast.67, bf16[1024,4,64]{0,2,1:T(8,128)(2,1)S(1)} %bitcast.60), kind=kOutput, calls=%fused_computation.7.clone.1 | convolution fusion | flops 175637760 | bytes 1118208 | tf_op jit(solution)/shard_map/while/body/eval_jaxpr/sub | solution.py:51
  77.8 3.1 %fusion.80 = bf16[256,4,64]{0,2,1:T(8,128)(2,1)S(1)} fusion(pred[256,1280]{1,0:T(8,128)(4,1)S(1)} %fusion.78, bf16[256,4,64]{0,2,1:T(8,128)(2,1)S(1)} %bitcast.69, bf16[1024,4,64]{0,2,1:T(8,128)(2,1)S(1)} %bitcast.62, bf16[256,4,64]{0,2,1:T(8,128)(2,1)} %bitcast.66, bf16[256,4,64]{0,2,1:T(8,128)(2,1)} %bitcast.68, ...), kind=kOutput, calls=%fused_computation.16.clone.1 | convolution fusion | flops 344852736 | bytes 1904640 | tf_op jit(solution)/shard_map/while/body/eval_jaxpr/hqk,khd->qhd/dot_general | solution.py:53
  81.8 1.4 %convolution_convert_fusion = bf16[512,1024]{1,0:T(8,128)(2,1)S(1)} fusion(bf16[512,256]{1,0:T(8,128)(2,1)} %bitcast.77, bf16[256,1024]{1,0:T(8,128)(2,1)S(1)} %copy-done), kind=kOutput, calls=%fused_computation.42 | convolution fusion | flops 268959744 | bytes 1835008 | tf_op jit(solution)/shard_map/dot_general | solution.py:86
  83.2 14.5 %all_to_all.26 = bf16[4,512,256]{2,1,0:T(8,128)(2,1)S(1)} all-to-all(bf16[4,512,256]{2,1,0:T(8,128)(2,1)S(1)} %bitcast.64), channel_id=1, replica_groups=mesh['req'=128,'tp'=4] {'tp'}, dimensions={0} | all-to-all | bytes 2097152 | tf_op jit(solution)/shard_map/all_to_all | solution.py:21
  99.9 3.4 %all-to-all-start.3 = ((f32[4,2,512]{2,1,0:T(2,128)}), f32[4,2,512]{2,1,0:T(2,128)S(1)}, u32[]{:S(2)}, u32[]{:S(2)}) async-start(f32[4,2,512]{2,1,0:T(2,128)} %broadcast_in_dim.84), calls=%async_computation.3 | async-start | bytes 32768 | tf_op jit(solution)/shard_map/all_to_all | solution.py:28
  104.9 2.5 %all-to-all-done.3 = f32[4,2,512]{2,1,0:T(2,128)S(1)} async-done(((f32[4,2,512]{2,1,0:T(2,128)}), f32[4,2,512]{2,1,0:T(2,128)S(1)}, u32[]{:S(2)}, u32[]{:S(2)}) %all-to-all-start.3) | async-done | bytes 16416 | tf_op jit(solution)/shard_map/all_to_all | solution.py:28
  107.7 1.1 add_convert_fusion
  108.7 11.9 %all-to-all-start.4 = ((bf16[128,4,256]{2,1,0:T(4,128)(2,1)}), bf16[128,4,256]{2,1,0:T(4,128)(2,1)S(1)}, u32[]{:S(2)}, u32[]{:S(2)}) async-start(bf16[128,4,256]{2,1,0:T(4,128)(2,1)} %add_convert_fusion), calls=%async_computation.4 | async-start | bytes 524288 | tf_op jit(solution)/shard_map/all_to_all | solution.py:125
  120.6 14.2 %all-to-all-done.4 = bf16[128,4,256]{2,1,0:T(4,128)(2,1)S(1)} async-done(((bf16[128,4,256]{2,1,0:T(4,128)(2,1)}), bf16[128,4,256]{2,1,0:T(4,128)(2,1)S(1)}, u32[]{:S(2)}, u32[]{:S(2)}) %all-to-all-start.4) | async-done | bytes 262176 | tf_op jit(solution)/shard_map/all_to_all | solution.py:125
  (83 shorter events, 16.4 us)
Async XLA Ops:
  0.0 81.8 %copy-start = (bf16[256,1024]{1,0:T(8,128)(2,1)S(1)}, bf16[256,1024]{1,0:T(8,128)(2,1)}, u32[]{:S(2)}) copy-start(bf16[256,1024]{1,0:T(8,128)(2,1)} %param.19) | copy-start | bytes 1572868
  36.1 1.3 copy-start.2
  37.4 17.4 %copy-start.8 = (bf16[1024,256]{1,0:T(8,128)(2,1)S(1)}, bf16[1024,256]{1,0:T(8,128)(2,1)}, u32[]{:S(2)}) copy-start(bf16[1024,256]{1,0:T(8,128)(2,1)} %param.18) | copy-start | bytes 1572868
  37.4 17.4 %all-to-all-start.1 = ((bf16[4,512,256]{1,2,0:T(8,128)(2,1)}), bf16[4,512,256]{1,2,0:T(8,128)(2,1)S(1)}, u32[]{:S(2)}, u32[]{:S(2)}) async-start(bf16[4,512,256]{1,2,0:T(8,128)(2,1)} %broadcast_in_dim.83), calls=%async_computation.1 | async-start | bytes 2097152 | tf_op jit(solution)/shard_map/all_to_all | solution.py:13
  54.8 1.2 copy-start.9
  56.0 1.2 copy-start.10
  57.2 1.2 copy-start.1
  57.2 1.2 copy-start.11
  62.4 2.5 %copy-start.4 = (bf16[1,256,256]{1,2,0:T(8,128)(2,1)}, bf16[1,256,256]{1,2,0:T(8,128)(2,1)S(1)}, u32[]{:S(2)}) copy-start(bf16[1,256,256]{1,2,0:T(8,128)(2,1)S(1)} %copy.77) | copy-start | bytes 393220 | tf_op jit(solution)/shard_map/while
  62.5 2.3 %copy-start.5 = (bf16[1,256,256]{1,2,0:T(8,128)(2,1)}, bf16[1,256,256]{1,2,0:T(8,128)(2,1)S(1)}, u32[]{:S(2)}) copy-start(bf16[1,256,256]{1,2,0:T(8,128)(2,1)S(1)} %copy.78) | copy-start | bytes 393220 | tf_op jit(solution)/shard_map/while
  66.1 3.3 %copy-start.6 = (bf16[2,256,256]{2,1,0:T(8,128)(2,1)S(1)}, bf16[2,256,256]{2,1,0:T(8,128)(2,1)}, u32[]{:S(2)}) copy-start(bf16[2,256,256]{2,1,0:T(8,128)(2,1)} %get-tuple-element.252) | copy-start | bytes 786436 | tf_op jit(solution)/shard_map/while
  69.4 0.7 copy-start.7
  74.0 2.5 %copy-start.4 = (bf16[1,256,256]{1,2,0:T(8,128)(2,1)}, bf16[1,256,256]{1,2,0:T(8,128)(2,1)S(1)}, u32[]{:S(2)}) copy-start(bf16[1,256,256]{1,2,0:T(8,128)(2,1)S(1)} %copy.77) | copy-start | bytes 393220 | tf_op jit(solution)/shard_map/while
  74.2 2.3 %copy-start.5 = (bf16[1,256,256]{1,2,0:T(8,128)(2,1)}, bf16[1,256,256]{1,2,0:T(8,128)(2,1)S(1)}, u32[]{:S(2)}) copy-start(bf16[1,256,256]{1,2,0:T(8,128)(2,1)S(1)} %copy.78) | copy-start | bytes 393220 | tf_op jit(solution)/shard_map/while
  77.8 3.3 %copy-start.6 = (bf16[2,256,256]{2,1,0:T(8,128)(2,1)S(1)}, bf16[2,256,256]{2,1,0:T(8,128)(2,1)}, u32[]{:S(2)}) copy-start(bf16[2,256,256]{2,1,0:T(8,128)(2,1)} %get-tuple-element.252) | copy-start | bytes 786436 | tf_op jit(solution)/shard_map/while
  81.0 0.7 copy-start.7
  97.7 1.0 copy-start.3
  99.9 7.4 %all-to-all-start.3 = ((f32[4,2,512]{2,1,0:T(2,128)}), f32[4,2,512]{2,1,0:T(2,128)S(1)}, u32[]{:S(2)}, u32[]{:S(2)}) async-start(f32[4,2,512]{2,1,0:T(2,128)} %broadcast_in_dim.84), calls=%async_computation.3 | async-start | bytes 32768 | tf_op jit(solution)/shard_map/all_to_all | solution.py:28
  108.7 26.1 %all-to-all-start.4 = ((bf16[128,4,256]{2,1,0:T(4,128)(2,1)}), bf16[128,4,256]{2,1,0:T(4,128)(2,1)S(1)}, u32[]{:S(2)}, u32[]{:S(2)}) async-start(bf16[128,4,256]{2,1,0:T(4,128)(2,1)} %add_convert_fusion), calls=%async_computation.4 | async-start | bytes 524288 | tf_op jit(solution)/shard_map/all_to_all | solution.py:125

commit v2 on v1

--- a/solution.py
+++ b/solution.py
@@ -60,18 +60,19 @@
 def attend_all(queries, new_keys, new_values, k_cache, v_cache, cache_len):
     request_count = k_cache.shape[0]
     req_shape = (request_count, queries.shape[0] // request_count, queries.shape[1])
-    context = lax.map(
-        lambda items: attend_padded(*items),
-        (
-            queries.reshape(req_shape),
-            new_keys.reshape(req_shape),
-            new_values.reshape(req_shape),
-            k_cache,
-            v_cache,
-            cache_len,
-        ),
-    )
-    return context.reshape(queries.shape)
+    span = req_shape[1]
+    parts = [
+        attend_padded(
+            queries[g * span:(g + 1) * span],
+            new_keys[g * span:(g + 1) * span],
+            new_values[g * span:(g + 1) * span],
+            k_cache[g],
+            v_cache[g],
+            cache_len[g],
+        )
+        for g in range(request_count)
+    ]
+    return jnp.concatenate(parts, 0)
 
 
 def project_rows(whole, w_query, w_key, w_value):

time: 137 us -> 125 us (0.912)
  blocking collectives: 47 us -> 14.4 us
  starting transfers between devices: 19.5 us -> 38.2 us
  waiting for transfers between devices: 29.9 us -> 37.7 us
  local copies, waits for them, and re-layouts: 19.6 us -> 15.2 us
  matrix products: 15.9 us -> 14.2 us
    all_to_all x1 -> x0, blocking collectives: 32.5 us -> none  [shards(): lax.all_to_all(to_blocks(tokens)[send_order], 'req', split_axis=0, concat...]
    all_to_all x0 -> x1, starting transfers between devices: none -> 18.4 us  [shards(): lax.all_to_all(to_blocks(tokens)[send_order], 'req', split_axis=0, concat...]
    all_to_all x0 -> x1, waiting for transfers between devices: none -> 10.4 us  [shards(): lax.all_to_all(to_blocks(tokens)[send_order], 'req', split_axis=0, concat...]
    dynamic_slice x18 -> x0, local copies, waits for them, and re-layouts: 8.77 us -> none  [attend_all(): lax.map(lambda items: attend_padded(*items), (queries.reshape(req_shape),...]
    slice x0 -> x10, local copies, waits for them, and re-layouts: none -> 5.27 us  [the longest x3 1.3 us: attend_all(): v_cache[g]]
    all_to_all x1, waiting for transfers between devices: 13.2 us -> 10.7 us  [gather_tp(): got = lax.all_to_all(copies, 'tp', 0, 0, tiled=True)]
    sub x2, matrix products: 4.66 us -> 6.83 us  [attend_padded(): weight = jnp.where(valid[None], jnp.exp(scores - top), 0.0)]
    while x16 -> x0, local copies, waits for them, and re-layouts: 1.42 us -> none
  transfers between devices with their start and end apart: 3 -> 4, of which waited for: 3 -> 4; matrix products, arithmetic and copies ran while one was open for 1% -> 6% of each run, Pallas kernels for 0% -> 0%
where the time goes in v2:
time: 125 us
  starting transfers between devices  38.2 us (31%)
  waiting for transfers between devices  37.7 us (30%)
  local copies, waits for them, and re-layouts  15.2 us (12%)
  blocking collectives  14.4 us (12%)
  matrix products  14.2 us (11%)
  other arithmetic  4.79 us (4%)
    all_to_all x1, starting transfers between devices, shards(): lax.all_to_all(to_blocks(tokens)[send_order], 'req', split_axis=0, concat...  18.4 us
    all_to_all x1, blocking collectives, scatter_sum_tp(): got = lax.all_to_all(pieces, 'tp', 0, 0, tiled=True)  14.4 us
    all_to_all x1, waiting for transfers between devices, shards(): lax.all_to_all(to_blocks(normed), 'req', split_axis=0, concat_axis=0, til...  14.2 us
    all_to_all x1, starting transfers between devices, shards(): lax.all_to_all(to_blocks(normed), 'req', split_axis=0, concat_axis=0, til...  12.1 us
    all_to_all x1, waiting for transfers between devices, gather_tp(): got = lax.all_to_all(copies, 'tp', 0, 0, tiled=True)  10.7 us
    all_to_all x1, waiting for transfers between devices, shards(): lax.all_to_all(to_blocks(tokens)[send_order], 'req', split_axis=0, concat...  10.4 us
    sub x2, matrix products, attend_padded(): weight = jnp.where(valid[None], jnp.exp(scores - top), 0.0)  6.83 us
    dot_general x2, matrix products, attend_padded(): jnp.einsum('hqk,khd->qhd', weight.astype(jnp.bfloat16), values_all, prefe...  5.51 us
  transfers between devices with their start and end apart: 4, of which 4 were waited for; matrix products, arithmetic and copies ran while one was open for 6% of the time, Pallas kernels for 0%

profile of v2, /device:TPU:1, one launch (start us, length us, event | category | flops | bytes accessed | tf_op | source)
XLA Modules:
  0.0 124.8 jit_solution(3557856080930325187)
XLA Ops:
  0.0 1.1 reshape.214
  1.8 1.0 scatter_custom_fusion
  2.8 1.5 %gather_fusion = bf16[128,4,256]{2,1,0:T(4,128)(2,1)} fusion(bf16[128,4,256]{2,1,0:T(4,128)(2,1)S(1)} %reshape.214, s32[1024]{0:T(1024)S(1)} %pad_clamp_fusion.1), kind=kCustom, calls=%fused_computation | custom fusion | bytes 524800 | tf_op jit(solution)/shard_map/gather | solution.py:120
  4.3 18.4 %all-to-all-start = ((bf16[128,4,256]{2,1,0:T(4,128)(2,1)}), bf16[128,4,256]{2,1,0:T(4,128)(2,1)S(1)}, u32[]{:S(2)}, u32[]{:S(2)}) async-start(bf16[128,4,256]{2,1,0:T(4,128)(2,1)} %gather_fusion), calls=%async_computation | async-start | bytes 524288 | tf_op jit(solution)/shard_map/all_to_all | solution.py:119
  22.9 1.0 copy.41
  24.3 1.0 copy.42
  26.6 10.4 %all-to-all-done = bf16[128,4,256]{2,1,0:T(4,128)(2,1)S(1)} async-done(((bf16[128,4,256]{2,1,0:T(4,128)(2,1)}), bf16[128,4,256]{2,1,0:T(4,128)(2,1)S(1)}, u32[]{:S(2)}, u32[]{:S(2)}) %all-to-all-start) | async-done | bytes 262176 | tf_op jit(solution)/shard_map/all_to_all | solution.py:119
  37.2 1.1 broadcast_in_dim.93
  38.3 4.1 %all-to-all-start.1 = ((bf16[4,512,256]{1,2,0:T(8,128)(2,1)}), bf16[4,512,256]{1,2,0:T(8,128)(2,1)S(1)}, u32[]{:S(2)}, u32[]{:S(2)}) async-start(bf16[4,512,256]{1,2,0:T(8,128)(2,1)} %broadcast_in_dim.93), calls=%async_computation.1 | async-start | bytes 2097152 | tf_op jit(solution)/shard_map/all_to_all | solution.py:13
  42.4 1.2 iota_compare_fusion.1
  43.7 1.2 fusion.17
  44.9 10.7 %all-to-all-done.1 = bf16[4,512,256]{1,2,0:T(8,128)(2,1)S(1)} async-done(((bf16[4,512,256]{1,2,0:T(8,128)(2,1)}), bf16[4,512,256]{1,2,0:T(8,128)(2,1)S(1)}, u32[]{:S(2)}, u32[]{:S(2)}) %all-to-all-start.1) | async-done | bytes 1048608 | tf_op jit(solution)/shard_map/all_to_all | solution.py:13
  59.1 3.5 %fusion.6 = f32[4,256]{1,0:T(4,128)S(1)} fusion(pred[256,1280]{1,0:T(8,128)(4,1)} %get-tuple-element.20, bf16[256,4,64]{0,2,1:T(8,128)(2,1)} %bitcast.68, bf16[256,4,64]{0,2,1:T(8,128)(2,1)S(1)} %bitcast.70, bf16[1024,4,64]{0,2,1:T(8,128)(2,1)S(1)} %bitcast.58), kind=kOutput, calls=%fused_computation.13 | convolution fusion | flops 175637760 | bytes 1118208 | tf_op jit(solution)/shard_map/sub | solution.py:51
  62.7 3.4 %fusion.27 = bf16[256,4,64]{0,2,1:T(8,128)(2,1)S(1)} fusion(pred[256,1280]{1,0:T(8,128)(4,1)} %get-tuple-element.20, bf16[256,4,64]{0,2,1:T(8,128)(2,1)} %bitcast.67, bf16[1024,4,64]{0,2,1:T(8,128)(2,1)S(1)} %bitcast.57, bf16[256,4,64]{0,2,1:T(8,128)(2,1)} %bitcast.69, bf16[256,4,64]{0,2,1:T(8,128)(2,1)} %bitcast.71, bf16[1024,4,64]{0,2,1:T(8,128)(2,1)S(1)} %bitcast.59, ...), kind=kOutput, calls=%fused_computation.32 | convolution fusion | flops 344852736 | bytes 1904640 | tf_op jit(solution)/shard_map/hqk,khd->qhd/dot_general | solution.py:53
  66.1 3.3 %fusion.4 = f32[4,256]{1,0:T(4,128)S(1)} fusion(pred[256,1280]{1,0:T(8,128)(4,1)S(1)} %copy-done.5, bf16[256,4,64]{0,2,1:T(8,128)(2,1)} %bitcast.63, bf16[256,4,64]{0,2,1:T(8,128)(2,1)} %bitcast.65, bf16[1024,4,64]{0,2,1:T(8,128)(2,1)S(1)} %bitcast.55), kind=kOutput, calls=%fused_computation.11 | convolution fusion | flops 175637760 | bytes 1118208 | tf_op jit(solution)/shard_map/sub | solution.py:51
  69.4 2.1 %fusion.33 = bf16[256,4,64]{0,2,1:T(8,128)(2,1)S(1)} fusion(pred[256,1280]{1,0:T(8,128)(4,1)S(1)} %copy-done.5, bf16[256,4,64]{0,2,1:T(8,128)(2,1)S(1)} %bitcast.62, bf16[1024,4,64]{0,2,1:T(8,128)(2,1)S(1)} %bitcast.54, bf16[256,4,64]{0,2,1:T(8,128)(2,1)S(1)} %bitcast.64, bf16[256,4,64]{0,2,1:T(8,128)(2,1)S(1)} %bitcast.66, ...), kind=kOutput, calls=%fused_computation.34 | convolution fusion | flops 344852736 | bytes 1904640 | tf_op jit(solution)/shard_map/hqk,khd->qhd/dot_general | solution.py:53
  72.1 14.4 %all_to_all.25 = bf16[4,512,256]{2,1,0:T(8,128)(2,1)S(1)} all-to-all(bf16[4,512,256]{2,1,0:T(8,128)(2,1)S(1)} %bitcast.50), channel_id=1, replica_groups=mesh['req'=128,'tp'=4] {'tp'}, dimensions={0} | all-to-all | bytes 2097152 | tf_op jit(solution)/shard_map/all_to_all | solution.py:21
  88.1 3.5 %all-to-all-start.3 = ((f32[4,2,512]{2,1,0:T(2,128)}), f32[4,2,512]{2,1,0:T(2,128)S(1)}, u32[]{:S(2)}, u32[]{:S(2)}) async-start(f32[4,2,512]{2,1,0:T(2,128)} %broadcast_in_dim.101), calls=%async_computation.3 | async-start | bytes 32768 | tf_op jit(solution)/shard_map/all_to_all | solution.py:28
  93.1 2.4 %all-to-all-done.3 = f32[4,2,512]{2,1,0:T(2,128)S(1)} async-done(((f32[4,2,512]{2,1,0:T(2,128)}), f32[4,2,512]{2,1,0:T(2,128)S(1)}, u32[]{:S(2)}, u32[]{:S(2)}) %all-to-all-start.3) | async-done | bytes 16416 | tf_op jit(solution)/shard_map/all_to_all | solution.py:28
  95.8 1.1 add_convert_fusion
  96.9 12.1 %all-to-all-start.4 = ((bf16[128,4,256]{2,1,0:T(4,128)(2,1)}), bf16[128,4,256]{2,1,0:T(4,128)(2,1)S(1)}, u32[]{:S(2)}, u32[]{:S(2)}) async-start(bf16[128,4,256]{2,1,0:T(4,128)(2,1)} %add_convert_fusion), calls=%async_computation.4 | async-start | bytes 524288 | tf_op jit(solution)/shard_map/all_to_all | solution.py:126
  109.0 14.2 %all-to-all-done.4 = bf16[128,4,256]{2,1,0:T(4,128)(2,1)S(1)} async-done(((bf16[128,4,256]{2,1,0:T(4,128)(2,1)}), bf16[128,4,256]{2,1,0:T(4,128)(2,1)S(1)}, u32[]{:S(2)}, u32[]{:S(2)}) %all-to-all-start.4) | async-done | bytes 262176 | tf_op jit(solution)/shard_map/all_to_all | solution.py:126
  123.2 0.8 gather_fusion.1
  124.1 0.8 reshape.219
  (62 shorter events, 10.1 us)
Async XLA Ops:
  0.0 71.5 %copy-start = (bf16[256,1024]{1,0:T(8,128)(2,1)S(1)}, bf16[256,1024]{1,0:T(8,128)(2,1)}, u32[]{:S(2)}) copy-start(bf16[256,1024]{1,0:T(8,128)(2,1)} %param.17) | copy-start | bytes 1572868
  0.0 22.8 %copy-start.1 = (bf16[2,1024,256]{2,1,0:T(8,128)(2,1)S(1)}, bf16[2,1024,256]{2,1,0:T(8,128)(2,1)}, u32[]{:S(2)}) copy-start(bf16[2,1024,256]{2,1,0:T(8,128)(2,1)} %param.19) | copy-start | bytes 3145732
  4.3 32.6 %all-to-all-start = ((bf16[128,4,256]{2,1,0:T(4,128)(2,1)}), bf16[128,4,256]{2,1,0:T(4,128)(2,1)S(1)}, u32[]{:S(2)}, u32[]{:S(2)}) async-start(bf16[128,4,256]{2,1,0:T(4,128)(2,1)} %gather_fusion), calls=%async_computation | async-start | bytes 524288 | tf_op jit(solution)/shard_map/all_to_all | solution.py:119
  22.8 1.4 %copy-start.2 = (bf16[2,1024,256]{2,1,0:T(8,128)(2,1)S(1)}, bf16[2,1024,256]{2,1,0:T(8,128)(2,1)}, u32[]{:S(2)}) copy-start(bf16[2,1024,256]{2,1,0:T(8,128)(2,1)} %param.18) | copy-start | bytes 3145732
  25.4 0.7 copy-start.9
  38.3 17.3 %copy-start.10 = (bf16[1024,256]{1,0:T(8,128)(2,1)S(1)}, bf16[1024,256]{1,0:T(8,128)(2,1)}, u32[]{:S(2)}) copy-start(bf16[1024,256]{1,0:T(8,128)(2,1)} %param.16) | copy-start | bytes 1572868
  38.3 17.3 %all-to-all-start.1 = ((bf16[4,512,256]{1,2,0:T(8,128)(2,1)}), bf16[4,512,256]{1,2,0:T(8,128)(2,1)S(1)}, u32[]{:S(2)}, u32[]{:S(2)}) async-start(bf16[4,512,256]{1,2,0:T(8,128)(2,1)} %broadcast_in_dim.93), calls=%async_computation.1 | async-start | bytes 2097152 | tf_op jit(solution)/shard_map/all_to_all | solution.py:13
  55.6 1.2 copy-start.11
  56.7 1.2 copy-start.12
  58.0 1.2 copy-start.4
  59.1 3.5 %copy-start.8 = (bf16[256,256]{0,1:T(8,128)(2,1)}, bf16[256,256]{0,1:T(8,128)(2,1)S(1)}, u32[]{:S(2)}) copy-start(bf16[256,256]{0,1:T(8,128)(2,1)S(1)} %get-tuple-element.14) | copy-start | bytes 393220
  59.1 3.5 %copy-start.3 = (bf16[1,1024,256]{1,2,0:T(8,128)(2,1)S(1)}, bf16[1,1024,256]{1,2,0:T(8,128)(2,1)}, u32[]{:S(2)}) copy-start(bf16[1,1024,256]{1,2,0:T(8,128)(2,1)} %copy.41) | copy-start | bytes 1572868
  62.7 3.4 %copy-start.5 = (pred[256,1280]{1,0:T(8,128)(4,1)S(1)}, pred[256,1280]{1,0:T(8,128)(4,1)}, u32[]{:S(2)}) copy-start(pred[256,1280]{1,0:T(8,128)(4,1)} %get-tuple-element.19) | copy-start | bytes 983044
  66.1 3.3 %copy-start.6 = (bf16[256,256]{0,1:T(8,128)(2,1)S(1)}, bf16[256,256]{0,1:T(8,128)(2,1)}, u32[]{:S(2)}) copy-start(bf16[256,256]{0,1:T(8,128)(2,1)} %get-tuple-element.15) | copy-start | bytes 393220
  66.1 3.3 %copy-start.7 = (bf16[256,256]{0,1:T(8,128)(2,1)S(1)}, bf16[256,256]{0,1:T(8,128)(2,1)}, u32[]{:S(2)}) copy-start(bf16[256,256]{0,1:T(8,128)(2,1)} %get-tuple-element.13) | copy-start | bytes 393220
  88.1 7.4 %all-to-all-start.3 = ((f32[4,2,512]{2,1,0:T(2,128)}), f32[4,2,512]{2,1,0:T(2,128)S(1)}, u32[]{:S(2)}, u32[]{:S(2)}) async-start(f32[4,2,512]{2,1,0:T(2,128)} %broadcast_in_dim.101), calls=%async_computation.3 | async-start | bytes 32768 | tf_op jit(solution)/shard_map/all_to_all | solution.py:28
  96.9 26.4 %all-to-all-start.4 = ((bf16[128,4,256]{2,1,0:T(4,128)(2,1)}), bf16[128,4,256]{2,1,0:T(4,128)(2,1)S(1)}, u32[]{:S(2)}, u32[]{:S(2)}) async-start(bf16[128,4,256]{2,1,0:T(4,128)(2,1)} %add_convert_fusion), calls=%async_computation.4 | async-start | bytes 524288 | tf_op jit(solution)/shard_map/all_to_all | solution.py:126

commit v3 on v2

--- a/solution.py
+++ b/solution.py
@@ -107,24 +107,26 @@
     block_rows = row_count // block_count
     per_peer = block_count // lax.axis_size("req")
     send_slot = placement // block_count * per_peer + placement % per_peer
-    send_order = (
-        jnp.zeros((block_count,), jnp.int32)
-        .at[send_slot]
-        .set(jnp.arange(block_count, dtype=jnp.int32))
-    )
+    choose = (
+        send_slot[None, :] == jnp.arange(block_count, dtype=jnp.int32)[:, None]
+    ).astype(jnp.bfloat16)
 
     def to_blocks(array):
         return array.reshape(block_count, block_rows, array.shape[1])
 
+    ordered = jnp.einsum(
+        "ja,aif->jif", choose, to_blocks(tokens), preferred_element_type=jnp.float32
+    ).astype(jnp.bfloat16)
     arrived = lax.all_to_all(
-        to_blocks(tokens)[send_order], "req", split_axis=0, concat_axis=0, tiled=True
+        ordered, "req", split_axis=0, concat_axis=0, tiled=True
     ).reshape(row_count, feat_width)
     whole = gather_tp(arrived)
     queries, new_keys, new_values = project_rows(whole, w_query, w_key, w_value)
     context = attend_all(queries, new_keys, new_values, k_cache, v_cache, cache_len)
     normed = finish_rows(context, arrived, w_out, ln_gain, ln_bias)
     returned = lax.all_to_all(to_blocks(normed), "req", split_axis=0, concat_axis=0, tiled=True)
-    return returned[send_slot].reshape(row_count, feat_width)
+    back = jnp.einsum("ja,jif->aif", choose, returned, preferred_element_type=jnp.float32)
+    return back.astype(jnp.bfloat16).reshape(row_count, feat_width)
 
 
 def solution(mesh):

time: 125 us -> 123 us (0.984)
  blocking collectives: 14.4 us -> 40.7 us
  waiting for transfers between devices: 37.7 us -> 23.5 us
  starting transfers between devices: 38.2 us -> 26 us
  local copies, waits for them, and re-layouts: 15.2 us -> 13 us
    all_to_all x0 -> x1, blocking collectives: none -> 26.3 us  [shards(): lax.all_to_all(to_blocks(normed), 'req', split_axis=0, concat_axis=0, til...]
    all_to_all x2 -> x1, waiting for transfers between devices: 24.6 us -> 10.4 us  [shards(): lax.all_to_all(ordered, 'req', split_axis=0, concat_axis=0, tiled=True)]
    all_to_all x2 -> x1, starting transfers between devices: 30.5 us -> 18.4 us  [shards(): lax.all_to_all(ordered, 'req', split_axis=0, concat_axis=0, tiled=True)]
    gather x2 -> x0, local copies, waits for them, and re-layouts: 2.35 us -> none  [the longest x1 1.52 us: shards(): to_blocks(tokens)[send_order]]
  transfers between devices with their start and end apart: 4 -> 3, of which waited for: 4 -> 3; matrix products, arithmetic and copies ran while one was open for 6% -> 6% of each run, Pallas kernels for 0% -> 0%
where the time goes in v3:
time: 123 us; the launch traced here: 122 us
  blocking collectives  40.7 us (33%)
  starting transfers between devices  26 us (21%)
  waiting for transfers between devices  23.5 us (19%)
  matrix products  14.8 us (12%)
  local copies, waits for them, and re-layouts  13 us (11%)
  other arithmetic  4.08 us (3%)
    all_to_all x1, blocking collectives, shards(): lax.all_to_all(to_blocks(normed), 'req', split_axis=0, concat_axis=0, til...  26.3 us
    all_to_all x1, starting transfers between devices, shards(): lax.all_to_all(ordered, 'req', split_axis=0, concat_axis=0, tiled=True)  18.4 us
    all_to_all x1, blocking collectives, scatter_sum_tp(): got = lax.all_to_all(pieces, 'tp', 0, 0, tiled=True)  14.4 us
    all_to_all x1, waiting for transfers between devices, gather_tp(): got = lax.all_to_all(copies, 'tp', 0, 0, tiled=True)  10.7 us
    all_to_all x1, waiting for transfers between devices, shards(): lax.all_to_all(ordered, 'req', split_axis=0, concat_axis=0, tiled=True)  10.4 us
    sub x2, matrix products, attend_padded(): weight = jnp.where(valid[None], jnp.exp(scores - top), 0.0)  6.82 us
    dot_general x2, matrix products, attend_padded(): jnp.einsum('hqk,khd->qhd', weight.astype(jnp.bfloat16), values_all, prefe...  5.51 us
    all_to_all x1, starting transfers between devices, gather_tp(): got = lax.all_to_all(copies, 'tp', 0, 0, tiled=True)  4.15 us
  transfers between devices with their start and end apart: 3, of which 3 were waited for; matrix products, arithmetic and copies ran while one was open for 6% of the time, Pallas kernels for 0%

profile of v3, /device:TPU:1, one launch (start us, length us, event | category | flops | bytes accessed | tf_op | source)
XLA Modules:
  0.0 122.4 jit_solution(13037040051344043849)
XLA Ops:
  0.0 1.1 reshape.215
  2.1 0.9 copy.62
  3.1 18.4 %all-to-all-start = ((bf16[128,4,256]{2,1,0:T(4,128)(2,1)}), bf16[128,4,256]{2,1,0:T(4,128)(2,1)S(1)}, u32[]{:S(2)}, u32[]{:S(2)}) async-start(bf16[128,4,256]{2,1,0:T(4,128)(2,1)} %copy.62), calls=%async_computation | async-start | bytes 524288 | tf_op jit(solution)/shard_map/all_to_all | solution.py:120
  21.6 1.0 copy.66
  23.1 1.0 copy.67
  25.3 10.4 %all-to-all-done = bf16[128,4,256]{2,1,0:T(4,128)(2,1)S(1)} async-done(((bf16[128,4,256]{2,1,0:T(4,128)(2,1)}), bf16[128,4,256]{2,1,0:T(4,128)(2,1)S(1)}, u32[]{:S(2)}, u32[]{:S(2)}) %all-to-all-start) | async-done | bytes 262176 | tf_op jit(solution)/shard_map/all_to_all | solution.py:120
  35.9 1.1 broadcast_in_dim.86
  37.0 4.1 %all-to-all-start.1 = ((bf16[4,512,256]{1,2,0:T(8,128)(2,1)}), bf16[4,512,256]{1,2,0:T(8,128)(2,1)S(1)}, u32[]{:S(2)}, u32[]{:S(2)}) async-start(bf16[4,512,256]{1,2,0:T(8,128)(2,1)} %broadcast_in_dim.86), calls=%async_computation.1 | async-start | bytes 2097152 | tf_op jit(solution)/shard_map/all_to_all | solution.py:13
  41.1 1.2 %iota_compare_fusion.2 = (pred[1280]{0:T(1024)(128)(4,1)S(1)}, pred[1280]{0:T(1024)(128)(4,1)S(1)}) fusion(s32[]{:T(128)} %bitcast.16, s32[]{:T(128)} %bitcast.6), kind=kLoop, calls=%fused_computation.61 | loop fusion | flops 2560 | bytes 2568 | tf_op jit(solution)/shard_map/lt | solution.py:48
  42.4 1.2 fusion.17
  43.6 10.7 %all-to-all-done.1 = bf16[4,512,256]{1,2,0:T(8,128)(2,1)S(1)} async-done(((bf16[4,512,256]{1,2,0:T(8,128)(2,1)}), bf16[4,512,256]{1,2,0:T(8,128)(2,1)S(1)}, u32[]{:S(2)}, u32[]{:S(2)}) %all-to-all-start.1) | async-done | bytes 1048608 | tf_op jit(solution)/shard_map/all_to_all | solution.py:13
  54.8 0.7 fusion.110
  55.9 0.7 fusion.109
  57.8 3.5 %fusion.6 = f32[4,256]{1,0:T(4,128)S(1)} fusion(pred[256,1280]{1,0:T(8,128)(4,1)} %get-tuple-element.20, bf16[256,4,64]{0,2,1:T(8,128)(2,1)} %bitcast.73, bf16[256,4,64]{0,2,1:T(8,128)(2,1)S(1)} %bitcast.75, bf16[1024,4,64]{0,2,1:T(8,128)(2,1)S(1)} %bitcast.63), kind=kOutput, calls=%fused_computation.10 | convolution fusion | flops 175637760 | bytes 1118208 | tf_op jit(solution)/shard_map/sub | solution.py:51
  61.4 3.4 %fusion.27 = bf16[256,4,64]{0,2,1:T(8,128)(2,1)S(1)} fusion(pred[256,1280]{1,0:T(8,128)(4,1)} %get-tuple-element.20, bf16[256,4,64]{0,2,1:T(8,128)(2,1)} %bitcast.72, bf16[1024,4,64]{0,2,1:T(8,128)(2,1)S(1)} %bitcast.62, bf16[256,4,64]{0,2,1:T(8,128)(2,1)} %bitcast.74, bf16[256,4,64]{0,2,1:T(8,128)(2,1)} %bitcast.76, bf16[1024,4,64]{0,2,1:T(8,128)(2,1)S(1)} %bitcast.64, ...), kind=kOutput, calls=%fused_computation.31 | convolution fusion | flops 344852736 | bytes 1904640 | tf_op jit(solution)/shard_map/hqk,khd->qhd/dot_general | solution.py:53
  64.8 3.3 %fusion.4 = f32[4,256]{1,0:T(4,128)S(1)} fusion(pred[256,1280]{1,0:T(8,128)(4,1)S(1)} %copy-done.5, bf16[256,4,64]{0,2,1:T(8,128)(2,1)} %bitcast.68, bf16[256,4,64]{0,2,1:T(8,128)(2,1)} %bitcast.70, bf16[1024,4,64]{0,2,1:T(8,128)(2,1)S(1)} %bitcast.60), kind=kOutput, calls=%fused_computation.8 | convolution fusion | flops 175637760 | bytes 1118208 | tf_op jit(solution)/shard_map/sub | solution.py:51
  68.1 2.1 %fusion.33 = bf16[256,4,64]{0,2,1:T(8,128)(2,1)S(1)} fusion(pred[256,1280]{1,0:T(8,128)(4,1)S(1)} %copy-done.5, bf16[256,4,64]{0,2,1:T(8,128)(2,1)S(1)} %bitcast.67, bf16[1024,4,64]{0,2,1:T(8,128)(2,1)S(1)} %bitcast.59, bf16[256,4,64]{0,2,1:T(8,128)(2,1)S(1)} %bitcast.69, bf16[256,4,64]{0,2,1:T(8,128)(2,1)S(1)} %bitcast.71, ...), kind=kOutput, calls=%fused_computation.33 | convolution fusion | flops 344852736 | bytes 1904640 | tf_op jit(solution)/shard_map/hqk,khd->qhd/dot_general | solution.py:53
  70.8 14.4 %all_to_all.25 = bf16[4,512,256]{2,1,0:T(8,128)(2,1)S(1)} all-to-all(bf16[4,512,256]{2,1,0:T(8,128)(2,1)S(1)} %bitcast.55), channel_id=1, replica_groups=mesh['req'=128,'tp'=4] {'tp'}, dimensions={0} | all-to-all | bytes 2097152 | tf_op jit(solution)/shard_map/all_to_all | solution.py:21
  86.8 3.5 %all-to-all-start.3 = ((f32[4,2,512]{2,1,0:T(2,128)}), f32[4,2,512]{2,1,0:T(2,128)S(1)}, u32[]{:S(2)}, u32[]{:S(2)}) async-start(f32[4,2,512]{2,1,0:T(2,128)} %broadcast_in_dim.94), calls=%async_computation.3 | async-start | bytes 32768 | tf_op jit(solution)/shard_map/all_to_all | solution.py:28
  90.3 0.8 dynamic_slice.7
  91.0 0.8 dynamic_slice.6
  91.8 2.4 %all-to-all-done.3 = f32[4,2,512]{2,1,0:T(2,128)S(1)} async-done(((f32[4,2,512]{2,1,0:T(2,128)}), f32[4,2,512]{2,1,0:T(2,128)S(1)}, u32[]{:S(2)}, u32[]{:S(2)}) %all-to-all-start.3) | async-done | bytes 16416 | tf_op jit(solution)/shard_map/all_to_all | solution.py:28
  94.9 26.3 %all_to_all.26 = bf16[128,4,256]{2,1,0:T(4,128)(2,1)S(1)} all-to-all(bf16[128,4,256]{2,1,0:T(4,128)(2,1)S(1)} %add_convert_fusion), channel_id=1, replica_groups=mesh['req'=128,'tp'=4] {'req'}, dimensions={0} | all-to-all | bytes 524288 | tf_op jit(solution)/shard_map/all_to_all | solution.py:127
  121.6 0.8 reshape.220
  (58 shorter events, 8.3 us)
Async XLA Ops:
  0.0 70.2 %copy-start = (bf16[256,1024]{1,0:T(8,128)(2,1)S(1)}, bf16[256,1024]{1,0:T(8,128)(2,1)}, u32[]{:S(2)}) copy-start(bf16[256,1024]{1,0:T(8,128)(2,1)} %param.17) | copy-start | bytes 1572868
  0.0 21.5 %copy-start.1 = (bf16[2,1024,256]{2,1,0:T(8,128)(2,1)S(1)}, bf16[2,1024,256]{2,1,0:T(8,128)(2,1)}, u32[]{:S(2)}) copy-start(bf16[2,1024,256]{2,1,0:T(8,128)(2,1)} %param.19) | copy-start | bytes 3145732
  3.1 32.6 %all-to-all-start = ((bf16[128,4,256]{2,1,0:T(4,128)(2,1)}), bf16[128,4,256]{2,1,0:T(4,128)(2,1)S(1)}, u32[]{:S(2)}, u32[]{:S(2)}) async-start(bf16[128,4,256]{2,1,0:T(4,128)(2,1)} %copy.62), calls=%async_computation | async-start | bytes 524288 | tf_op jit(solution)/shard_map/all_to_all | solution.py:120
  21.6 1.4 %copy-start.2 = (bf16[2,1024,256]{2,1,0:T(8,128)(2,1)S(1)}, bf16[2,1024,256]{2,1,0:T(8,128)(2,1)}, u32[]{:S(2)}) copy-start(bf16[2,1024,256]{2,1,0:T(8,128)(2,1)} %param.18) | copy-start | bytes 3145732
  24.1 0.7 copy-start.9
  37.0 17.3 %copy-start.10 = (bf16[1024,256]{1,0:T(8,128)(2,1)S(1)}, bf16[1024,256]{1,0:T(8,128)(2,1)}, u32[]{:S(2)}) copy-start(bf16[1024,256]{1,0:T(8,128)(2,1)} %param.16) | copy-start | bytes 1572868
  37.0 17.3 %all-to-all-start.1 = ((bf16[4,512,256]{1,2,0:T(8,128)(2,1)}), bf16[4,512,256]{1,2,0:T(8,128)(2,1)S(1)}, u32[]{:S(2)}, u32[]{:S(2)}) async-start(bf16[4,512,256]{1,2,0:T(8,128)(2,1)} %broadcast_in_dim.86), calls=%async_computation.1 | async-start | bytes 2097152 | tf_op jit(solution)/shard_map/all_to_all | solution.py:13
  54.3 1.2 copy-start.11
  55.5 1.2 copy-start.12
  56.7 1.2 copy-start.4
  57.8 3.5 %copy-start.8 = (bf16[256,256]{0,1:T(8,128)(2,1)}, bf16[256,256]{0,1:T(8,128)(2,1)S(1)}, u32[]{:S(2)}) copy-start(bf16[256,256]{0,1:T(8,128)(2,1)S(1)} %get-tuple-element.14) | copy-start | bytes 393220
  57.8 3.5 %copy-start.3 = (bf16[1,1024,256]{1,2,0:T(8,128)(2,1)S(1)}, bf16[1,1024,256]{1,2,0:T(8,128)(2,1)}, u32[]{:S(2)}) copy-start(bf16[1,1024,256]{1,2,0:T(8,128)(2,1)} %copy.66) | copy-start | bytes 1572868
  61.4 3.4 %copy-start.5 = (pred[256,1280]{1,0:T(8,128)(4,1)S(1)}, pred[256,1280]{1,0:T(8,128)(4,1)}, u32[]{:S(2)}) copy-start(pred[256,1280]{1,0:T(8,128)(4,1)} %get-tuple-element.19) | copy-start | bytes 983044
  64.8 3.3 %copy-start.6 = (bf16[256,256]{0,1:T(8,128)(2,1)S(1)}, bf16[256,256]{0,1:T(8,128)(2,1)}, u32[]{:S(2)}) copy-start(bf16[256,256]{0,1:T(8,128)(2,1)} %get-tuple-element.15) | copy-start | bytes 393220
  64.8 3.3 %copy-start.7 = (bf16[256,256]{0,1:T(8,128)(2,1)S(1)}, bf16[256,256]{0,1:T(8,128)(2,1)}, u32[]{:S(2)}) copy-start(bf16[256,256]{0,1:T(8,128)(2,1)} %get-tuple-element.13) | copy-start | bytes 393220
  86.8 7.4 %all-to-all-start.3 = ((f32[4,2,512]{2,1,0:T(2,128)}), f32[4,2,512]{2,1,0:T(2,128)S(1)}, u32[]{:S(2)}, u32[]{:S(2)}) async-start(f32[4,2,512]{2,1,0:T(2,128)} %broadcast_in_dim.94), calls=%async_computation.3 | async-start | bytes 32768 | tf_op jit(solution)/shard_map/all_to_all | solution.py:28

commit v4 on v3

--- a/solution.py
+++ b/solution.py
@@ -1,6 +1,8 @@
 import jax
 import jax.numpy as jnp
 from jax import lax
+from jax.experimental import pallas as pl
+from jax.experimental.pallas import tpu as pltpu
 from jax.sharding import PartitionSpec as P
 
 D = 1024
@@ -27,6 +29,57 @@
     copies = jnp.broadcast_to(stats[None], (count,) + stats.shape)
     got = lax.all_to_all(copies, "tp", 0, 0, tiled=True)
     return jnp.sum(got, axis=0)
+
+
+HEAD = 64
+
+
+def attend_kernel(lens_ref, q_ref, kn_ref, vn_ref, kc_ref, vc_ref, out_ref):
+    g = pl.program_id(0)
+    length = lens_ref[g]
+    new_count = q_ref.shape[1]
+    span = kc_ref.shape[1]
+    heads = q_ref.shape[2] // HEAD
+    cache_pos = lax.broadcasted_iota(jnp.int32, (new_count, span), 1)
+    cache_ok = cache_pos < length
+    row = lax.broadcasted_iota(jnp.int32, (new_count, new_count), 0)
+    col = lax.broadcasted_iota(jnp.int32, (new_count, new_count), 1)
+    new_ok = col <= row
+    dims = (((1,), (1,)), ((), ()))
+    for h in range(heads):
+        cols = slice(h * HEAD, (h + 1) * HEAD)
+        qh = q_ref[0, :, cols]
+        sc = lax.dot_general(qh, kc_ref[0, :, cols], dims, preferred_element_type=jnp.float32) * HEAD ** (-0.5)
+        sn = lax.dot_general(qh, kn_ref[0, :, cols], dims, preferred_element_type=jnp.float32) * HEAD ** (-0.5)
+        sc = jnp.where(cache_ok, sc, -jnp.inf)
+        sn = jnp.where(new_ok, sn, -jnp.inf)
+        top = jnp.maximum(jnp.max(sc, axis=1, keepdims=True), jnp.max(sn, axis=1, keepdims=True))
+        wc = jnp.where(cache_ok, jnp.exp(sc - top), 0.0)
+        wn = jnp.where(new_ok, jnp.exp(sn - top), 0.0)
+        total = jnp.sum(wc, axis=1, keepdims=True) + jnp.sum(wn, axis=1, keepdims=True)
+        ctx = jnp.dot(wc.astype(jnp.bfloat16), vc_ref[0, :, cols], preferred_element_type=jnp.float32)
+        ctx = ctx + jnp.dot(wn.astype(jnp.bfloat16), vn_ref[0, :, cols], preferred_element_type=jnp.float32)
+        out_ref[0, :, cols] = (ctx / total).astype(out_ref.dtype)
+
+
+def attend_pallas(queries, new_keys, new_values, k_cache, v_cache, cache_len):
+    requests, span, width = k_cache.shape
+    new_count = queries.shape[0] // requests
+    shape3 = (requests, new_count, width)
+    q3, kn3, vn3 = (a.reshape(shape3) for a in (queries, new_keys, new_values))
+    new_spec = pl.BlockSpec((1, new_count, width), lambda g, lens: (g, 0, 0))
+    cache_spec = pl.BlockSpec((1, span, width), lambda g, lens: (g, 0, 0))
+    out = pl.pallas_call(
+        attend_kernel,
+        out_shape=jax.ShapeDtypeStruct(shape3, jnp.bfloat16),
+        grid_spec=pltpu.PrefetchScalarGridSpec(
+            num_scalar_prefetch=1,
+            grid=(requests,),
+            in_specs=[new_spec, new_spec, new_spec, cache_spec, cache_spec],
+            out_specs=new_spec,
+        ),
+    )(cache_len, q3, kn3, vn3, k_cache, v_cache)
+    return out.reshape(queries.shape)
 
 
 def head_view(array, head_size):
@@ -122,7 +175,7 @@
     ).reshape(row_count, feat_width)
     whole = gather_tp(arrived)
     queries, new_keys, new_values = project_rows(whole, w_query, w_key, w_value)
-    context = attend_all(queries, new_keys, new_values, k_cache, v_cache, cache_len)
+    context = attend_pallas(queries, new_keys, new_values, k_cache, v_cache, cache_len)
     normed = finish_rows(context, arrived, w_out, ln_gain, ln_bias)
     returned = lax.all_to_all(to_blocks(normed), "req", split_axis=0, concat_axis=0, tiled=True)
     back = jnp.einsum("ja,jif->aif", choose, returned, preferred_element_type=jnp.float32)

time: 123 us -> 117 us (0.951)
  blocking collectives: 40.7 us -> 89.9 us
  starting transfers between devices: 26 us -> 3.25 us
  waiting for transfers between devices: 23.5 us -> 2.65 us
  matrix products: 14.8 us -> 5.54 us
  Pallas kernels: 0 us -> 7.9 us
  local copies, waits for them, and re-layouts: 13 us -> 5.27 us
  other arithmetic: 4.08 us -> 1.7 us
    all_to_all x0 -> x2, blocking collectives: none -> 49.7 us  [the longest x1 32.5 us: shards(): lax.all_to_all(ordered, 'req', split_axis=0, concat_axis=0, tiled=True)]
    all_to_all x2 -> x0, starting transfers between devices: 22.6 us -> none  [the longest x1 18.4 us: shards(): lax.all_to_all(ordered, 'req', split_axis=0, concat_axis=0, tiled=True)]
    all_to_all x2 -> x0, waiting for transfers between devices: 21.1 us -> none  [the longest x1 10.7 us: gather_tp(): got = lax.all_to_all(copies, 'tp', 0, 0, tiled=True)]
    pallas_call x0 -> x1, Pallas kernels: none -> 7.9 us  [attend_pallas(): pl.pallas_call(attend_kernel, out_shape=jax.ShapeDtypeStruct(shape3, jnp....]
    sub x2 -> x0, matrix products: 6.82 us -> none  [attend_padded(): weight = jnp.where(valid[None], jnp.exp(scores - top), 0.0)]
    dot_general x2 -> x0, matrix products: 5.51 us -> none  [attend_padded(): jnp.einsum('hqk,khd->qhd', weight.astype(jnp.bfloat16), values_all, prefe...]
    slice x10 -> x0, local copies, waits for them, and re-layouts: 5.27 us -> none  [the longest x3 1.3 us: attend_all(): v_cache[g]]
  transfers between devices with their start and end apart: 3 -> 1, of which waited for: 3 -> 1; matrix products, arithmetic and copies ran while one was open for 6% -> 1% of each run, Pallas kernels for 0% -> 0%
where the time goes in v4:
time: 117 us; the launch traced here: 116 us
  blocking collectives  89.9 us (77%)
  Pallas kernels  7.9 us (7%)
  matrix products  5.54 us (5%)
  local copies, waits for them, and re-layouts  5.27 us (5%)
  starting transfers between devices  3.25 us (3%)
  waiting for transfers between devices  2.65 us (2%)
  other arithmetic  1.7 us (1%)
    all_to_all x1, blocking collectives, shards(): lax.all_to_all(ordered, 'req', split_axis=0, concat_axis=0, tiled=True)  32.5 us
    all_to_all x1, blocking collectives, shards(): lax.all_to_all(to_blocks(normed), 'req', split_axis=0, concat_axis=0, til...  25.7 us
    all_to_all x1, blocking collectives, gather_tp(): got = lax.all_to_all(copies, 'tp', 0, 0, tiled=True)  17.2 us
    all_to_all x1, blocking collectives, scatter_sum_tp(): got = lax.all_to_all(pieces, 'tp', 0, 0, tiled=True)  14.5 us
    pallas_call x1, Pallas kernels, attend_pallas(): pl.pallas_call(attend_kernel, out_shape=jax.ShapeDtypeStruct(shape3, jnp....  7.9 us
    all_to_all x1, starting transfers between devices, sum_tp(): got = lax.all_to_all(copies, 'tp', 0, 0, tiled=True)  3.25 us
    all_to_all x1, waiting for transfers between devices, sum_tp(): got = lax.all_to_all(copies, 'tp', 0, 0, tiled=True)  2.65 us
  transfers between devices with their start and end apart: 1, of which 1 were waited for; matrix products, arithmetic and copies ran while one was open for 1% of the time, Pallas kernels for 0%

profile of v4, /device:TPU:1, one launch (start us, length us, event | category | flops | bytes accessed | tf_op | source)
XLA Modules:
  0.0 116.4 jit_solution(10434512115783320104)
XLA Ops:
  0.0 0.7 and_select_fusion
  0.7 1.0 reshape.81
  1.7 0.3 convolution_convert_fusion.5
  2.1 0.2 copy.46
  2.3 32.5 %all_to_all.25 = bf16[128,4,256]{2,1,0:T(4,128)(2,1)S(1)} all-to-all(bf16[128,4,256]{2,1,0:T(4,128)(2,1)S(1)} %copy.46), channel_id=1, replica_groups=mesh['req'=128,'tp'=4] {'req'}, dimensions={0} | all-to-all | bytes 524288 | tf_op jit(solution)/shard_map/all_to_all | solution.py:173
  35.1 17.2 %all_to_all.26 = bf16[4,512,256]{1,2,0:T(8,128)(2,1)S(1)} all-to-all(bf16[4,512,256]{1,2,0:T(8,128)(2,1)S(1)} %broadcast_in_dim.7), channel_id=1, replica_groups=mesh['req'=128,'tp'=4] {'tp'}, dimensions={0} | all-to-all | bytes 2097152 | tf_op jit(solution)/shard_map/all_to_all | solution.py:15
  52.3 1.2 %convolution_convert_fusion.4 = bf16[512,256]{1,0:T(8,128)(2,1)} fusion(bf16[512,1024]{0,1:T(8,128)(2,1)S(1)} %bitcast.29, bf16[1024,256]{1,0:T(8,128)(2,1)S(1)} %copy-done.1), kind=kOutput, calls=%fused_computation.5 | convolution fusion | flops 268566528 | bytes 1835008 | tf_op jit(solution)/shard_map/dot_general | solution.py:132
  53.5 1.2 %convolution_convert_fusion.3 = bf16[512,256]{1,0:T(8,128)(2,1)} fusion(bf16[512,1024]{0,1:T(8,128)(2,1)S(1)} %bitcast.30, bf16[1024,256]{1,0:T(8,128)(2,1)S(1)} %copy-done.2), kind=kOutput, calls=%fused_computation.4 | convolution fusion | flops 268566528 | bytes 1835008 | tf_op jit(solution)/shard_map/dot_general | solution.py:133
  54.7 1.2 %convolution_convert_fusion.2 = bf16[512,256]{1,0:T(8,128)(2,1)} fusion(bf16[512,1024]{0,1:T(8,128)(2,1)S(1)} %bitcast.31, bf16[1024,256]{1,0:T(8,128)(2,1)S(1)} %copy-done.3), kind=kOutput, calls=%fused_computation.3 | convolution fusion | flops 268566528 | bytes 1835008 | tf_op jit(solution)/shard_map/dot_general | solution.py:134
  55.9 7.9 %shard_map.109 = bf16[2,256,256]{2,1,0:T(8,128)(2,1)} custom-call(s32[2]{0:T(128)} %lens_ref.1, bf16[2,256,256]{2,1,0:T(8,128)(2,1)} %bitcast.33, bf16[2,256,256]{2,1,0:T(8,128)(2,1)} %bitcast.34, bf16[2,256,256]{2,1,0:T(8,128)(2,1)} %bitcast.35, bf16[2,1024,256]{2,1,0:T(8,128)(2,1)} %kc_ref.1, bf16[2,1024,256]{2,1,0:T(8,128)(2,1)} %vc_ref.1), custom_call_target="tpu_custom_call" | custom-call | tf_op jit(solution)/shard_map/pallas_call | solution.py:72
  63.8 1.4 %convolution_convert_fusion = bf16[512,1024]{1,0:T(8,128)(2,1)S(1)} fusion(bf16[512,256]{1,0:T(8,128)(2,1)} %bitcast.32, bf16[256,1024]{1,0:T(8,128)(2,1)S(1)} %copy-done), kind=kOutput, calls=%fused_computation.1 | convolution fusion | flops 268959744 | bytes 1835008 | tf_op jit(solution)/shard_map/dot_general | solution.py:140
  65.3 14.5 %all_to_all.27 = bf16[4,512,256]{2,1,0:T(8,128)(2,1)S(1)} all-to-all(bf16[4,512,256]{2,1,0:T(8,128)(2,1)S(1)} %bitcast.28), channel_id=1, replica_groups=mesh['req'=128,'tp'=4] {'tp'}, dimensions={0} | all-to-all | bytes 2097152 | tf_op jit(solution)/shard_map/all_to_all | solution.py:23
  79.9 0.1 reduce_sum.39
  80.1 0.4 fusion.2
  80.7 0.6 broadcast_in_dim.8
  81.3 3.3 %all-to-all-start.3 = ((f32[4,2,512]{2,1,0:T(2,128)}), f32[4,2,512]{2,1,0:T(2,128)S(1)}, u32[]{:S(2)}, u32[]{:S(2)}) async-start(f32[4,2,512]{2,1,0:T(2,128)} %broadcast_in_dim.8), calls=%async_computation.3 | async-start | bytes 32768 | tf_op jit(solution)/shard_map/all_to_all | solution.py:30
  84.6 0.8 dynamic_slice.6
  85.4 0.8 dynamic_slice.7
  86.1 2.6 %all-to-all-done.3 = f32[4,2,512]{2,1,0:T(2,128)S(1)} async-done(((f32[4,2,512]{2,1,0:T(2,128)}), f32[4,2,512]{2,1,0:T(2,128)S(1)}, u32[]{:S(2)}, u32[]{:S(2)}) %all-to-all-start.3) | async-done | bytes 16416 | tf_op jit(solution)/shard_map/all_to_all | solution.py:30
  89.1 0.4 add_convert_fusion
  89.4 25.7 %all_to_all.28 = bf16[128,4,256]{2,1,0:T(4,128)(2,1)S(1)} all-to-all(bf16[128,4,256]{2,1,0:T(4,128)(2,1)S(1)} %add_convert_fusion), channel_id=1, replica_groups=mesh['req'=128,'tp'=4] {'req'}, dimensions={0} | all-to-all | bytes 524288 | tf_op jit(solution)/shard_map/all_to_all | solution.py:180
  115.1 0.3 convolution_convert_fusion.1
  115.4 0.2 copy.55
  115.6 0.8 reshape.88
  (21 shorter events, 1.0 us)
Async XLA Ops:
  0.0 63.8 %copy-start = (bf16[256,1024]{1,0:T(8,128)(2,1)S(1)}, bf16[256,1024]{1,0:T(8,128)(2,1)}, u32[]{:S(2)}) copy-start(bf16[256,1024]{1,0:T(8,128)(2,1)} %param.17) | copy-start | bytes 1572868
  35.1 17.2 %copy-start.1 = (bf16[1024,256]{1,0:T(8,128)(2,1)S(1)}, bf16[1024,256]{1,0:T(8,128)(2,1)}, u32[]{:S(2)}) copy-start(bf16[1024,256]{1,0:T(8,128)(2,1)} %param.14) | copy-start | bytes 1572868
  52.3 1.2 %copy-start.2 = (bf16[1024,256]{1,0:T(8,128)(2,1)S(1)}, bf16[1024,256]{1,0:T(8,128)(2,1)}, u32[]{:S(2)}) copy-start(bf16[1024,256]{1,0:T(8,128)(2,1)} %param.15) | copy-start | bytes 1572868
  53.5 1.2 %copy-start.3 = (bf16[1024,256]{1,0:T(8,128)(2,1)S(1)}, bf16[1024,256]{1,0:T(8,128)(2,1)}, u32[]{:S(2)}) copy-start(bf16[1024,256]{1,0:T(8,128)(2,1)} %param.16) | copy-start | bytes 1572868
  81.3 7.4 %all-to-all-start.3 = ((f32[4,2,512]{2,1,0:T(2,128)}), f32[4,2,512]{2,1,0:T(2,128)S(1)}, u32[]{:S(2)}, u32[]{:S(2)}) async-start(f32[4,2,512]{2,1,0:T(2,128)} %broadcast_in_dim.8), calls=%async_computation.3 | async-start | bytes 32768 | tf_op jit(solution)/shard_map/all_to_all | solution.py:30

commit v5 on v4

--- a/solution.py
+++ b/solution.py
@@ -54,8 +54,8 @@
         sc = jnp.where(cache_ok, sc, -jnp.inf)
         sn = jnp.where(new_ok, sn, -jnp.inf)
         top = jnp.maximum(jnp.max(sc, axis=1, keepdims=True), jnp.max(sn, axis=1, keepdims=True))
-        wc = jnp.where(cache_ok, jnp.exp(sc - top), 0.0)
-        wn = jnp.where(new_ok, jnp.exp(sn - top), 0.0)
+        wc = jnp.exp(sc - top)
+        wn = jnp.exp(sn - top)
         total = jnp.sum(wc, axis=1, keepdims=True) + jnp.sum(wn, axis=1, keepdims=True)
         ctx = jnp.dot(wc.astype(jnp.bfloat16), vc_ref[0, :, cols], preferred_element_type=jnp.float32)
         ctx = ctx + jnp.dot(wn.astype(jnp.bfloat16), vn_ref[0, :, cols], preferred_element_type=jnp.float32)
@@ -129,10 +129,10 @@
 
 
 def project_rows(whole, w_query, w_key, w_value):
-    queries = jnp.dot(whole, w_query, preferred_element_type=jnp.float32).astype(jnp.bfloat16)
-    new_keys = jnp.dot(whole, w_key, preferred_element_type=jnp.float32).astype(jnp.bfloat16)
-    new_values = jnp.dot(whole, w_value, preferred_element_type=jnp.float32).astype(jnp.bfloat16)
-    return (queries, new_keys, new_values)
+    width = w_query.shape[1]
+    joined = jnp.concatenate([w_query, w_key, w_value], 1)
+    all_three = jnp.dot(whole, joined, preferred_element_type=jnp.float32).astype(jnp.bfloat16)
+    return (all_three[:, :width], all_three[:, width:2 * width], all_three[:, 2 * width:])
 
 
 def finish_rows(context, local, w_out, ln_gain, ln_bias):

time: 117 us -> 115 us (0.983)
  matrix products: 5.54 us -> 3.02 us
    dot_general x3 -> x1, matrix products: 3.55 us -> 1.04 us  [project_rows(): jnp.dot(whole, joined, preferred_element_type=jnp.float32)]
where the time goes in v5:
time: 115 us
  blocking collectives  89.9 us (78%)
  Pallas kernels  7.78 us (7%)
  local copies, waits for them, and re-layouts  6.16 us (5%)
  starting transfers between devices  3.25 us (3%)
  matrix products  3.02 us (3%)
  waiting for transfers between devices  2.65 us (2%)
  other arithmetic  1.7 us (1%)
    all_to_all x1, blocking collectives, shards(): lax.all_to_all(ordered, 'req', split_axis=0, concat_axis=0, tiled=True)  32.5 us
    all_to_all x1, blocking collectives, shards(): lax.all_to_all(to_blocks(normed), 'req', split_axis=0, concat_axis=0, til...  25.7 us
    all_to_all x1, blocking collectives, gather_tp(): got = lax.all_to_all(copies, 'tp', 0, 0, tiled=True)  17.2 us
    all_to_all x1, blocking collectives, scatter_sum_tp(): got = lax.all_to_all(pieces, 'tp', 0, 0, tiled=True)  14.5 us
    pallas_call x1, Pallas kernels, attend_pallas(): pl.pallas_call(attend_kernel, out_shape=jax.ShapeDtypeStruct(shape3, jnp....  7.78 us
    all_to_all x1, starting transfers between devices, sum_tp(): got = lax.all_to_all(copies, 'tp', 0, 0, tiled=True)  3.25 us
    all_to_all x1, waiting for transfers between devices, sum_tp(): got = lax.all_to_all(copies, 'tp', 0, 0, tiled=True)  2.65 us
  transfers between devices with their start and end apart: 1, of which 1 were waited for; matrix products, arithmetic and copies ran while one was open for 1% of the time, Pallas kernels for 0%

profile of v5, /device:TPU:1, one launch (start us, length us, event | category | flops | bytes accessed | tf_op | source)
XLA Modules:
  0.0 114.7 jit_solution(532494461004967131)
XLA Ops:
  0.0 0.7 and_select_fusion
  0.7 1.0 reshape.81
  1.7 0.3 convolution_convert_fusion.2
  2.1 0.2 copy.46
  2.3 32.5 %all_to_all.25 = bf16[128,4,256]{2,1,0:T(4,128)(2,1)S(1)} all-to-all(bf16[128,4,256]{2,1,0:T(4,128)(2,1)S(1)} %copy.46), channel_id=1, replica_groups=mesh['req'=128,'tp'=4] {'req'}, dimensions={0} | all-to-all | bytes 524288 | tf_op jit(solution)/shard_map/all_to_all | solution.py:173
  35.2 17.2 %all_to_all.26 = bf16[4,512,256]{1,2,0:T(8,128)(2,1)S(1)} all-to-all(bf16[4,512,256]{1,2,0:T(8,128)(2,1)S(1)} %broadcast_in_dim.7), channel_id=1, replica_groups=mesh['req'=128,'tp'=4] {'tp'}, dimensions={0} | all-to-all | bytes 2097152 | tf_op jit(solution)/shard_map/all_to_all | solution.py:15
  52.4 1.0 fusion.6
  53.4 0.9 fusion.20
  54.3 7.8 %shard_map.109 = bf16[2,256,256]{2,1,0:T(8,128)(2,1)} custom-call(s32[2]{0:T(128)} %lens_ref.1, bf16[2,256,256]{2,1,0:T(8,128)(2,1)} %bitcast.28, bf16[2,256,256]{2,1,0:T(8,128)(2,1)} %bitcast.27, bf16[2,256,256]{2,1,0:T(8,128)(2,1)} %bitcast.26, bf16[2,1024,256]{2,1,0:T(8,128)(2,1)} %kc_ref.1, bf16[2,1024,256]{2,1,0:T(8,128)(2,1)} %vc_ref.1), custom_call_target="tpu_custom_call" | custom-call | tf_op jit(solution)/shard_map/pallas_call | solution.py:72
  62.1 1.4 %convolution_convert_fusion = bf16[512,1024]{1,0:T(8,128)(2,1)S(1)} fusion(bf16[512,256]{1,0:T(8,128)(2,1)} %bitcast.25, bf16[256,1024]{1,0:T(8,128)(2,1)S(1)} %copy-done), kind=kOutput, calls=%fused_computation.7 | convolution fusion | flops 268959744 | bytes 1835008 | tf_op jit(solution)/shard_map/dot_general | solution.py:140
  63.5 14.5 %all_to_all.27 = bf16[4,512,256]{2,1,0:T(8,128)(2,1)S(1)} all-to-all(bf16[4,512,256]{2,1,0:T(8,128)(2,1)S(1)} %bitcast.23), channel_id=1, replica_groups=mesh['req'=128,'tp'=4] {'tp'}, dimensions={0} | all-to-all | bytes 2097152 | tf_op jit(solution)/shard_map/all_to_all | solution.py:23
  78.1 0.1 convert_reduce_fusion
  78.2 0.1 reduce_sum.39
  78.4 0.4 fusion.11
  79.0 0.6 broadcast_in_dim.8
  79.6 3.3 %all-to-all-start.3 = ((f32[4,2,512]{2,1,0:T(2,128)}), f32[4,2,512]{2,1,0:T(2,128)S(1)}, u32[]{:S(2)}, u32[]{:S(2)}) async-start(f32[4,2,512]{2,1,0:T(2,128)} %broadcast_in_dim.8), calls=%async_computation.3 | async-start | bytes 32768 | tf_op jit(solution)/shard_map/all_to_all | solution.py:30
  82.9 0.8 dynamic_slice.6
  83.6 0.8 dynamic_slice.7
  84.4 2.6 %all-to-all-done.3 = f32[4,2,512]{2,1,0:T(2,128)S(1)} async-done(((f32[4,2,512]{2,1,0:T(2,128)}), f32[4,2,512]{2,1,0:T(2,128)S(1)}, u32[]{:S(2)}, u32[]{:S(2)}) %all-to-all-start.3) | async-done | bytes 16416 | tf_op jit(solution)/shard_map/all_to_all | solution.py:30
  87.3 0.4 add_convert_fusion
  87.7 25.7 %all_to_all.28 = bf16[128,4,256]{2,1,0:T(4,128)(2,1)S(1)} all-to-all(bf16[128,4,256]{2,1,0:T(4,128)(2,1)S(1)} %add_convert_fusion), channel_id=1, replica_groups=mesh['req'=128,'tp'=4] {'req'}, dimensions={0} | all-to-all | bytes 524288 | tf_op jit(solution)/shard_map/all_to_all | solution.py:180
  113.4 0.3 convolution_convert_fusion.1
  113.7 0.2 copy.55
  113.9 0.8 reshape.88
  (20 shorter events, 0.9 us)
Async XLA Ops:
  0.0 62.1 %copy-start = (bf16[256,1024]{1,0:T(8,128)(2,1)S(1)}, bf16[256,1024]{1,0:T(8,128)(2,1)}, u32[]{:S(2)}) copy-start(bf16[256,1024]{1,0:T(8,128)(2,1)} %param.17) | copy-start | bytes 1572868
  35.1 17.2 %copy-start.1 = (bf16[1024,256]{1,0:T(8,128)(2,1)S(1)}, bf16[1024,256]{1,0:T(8,128)(2,1)}, u32[]{:S(2)}) copy-start(bf16[1024,256]{1,0:T(8,128)(2,1)} %param.16) | copy-start | bytes 1572868
  35.1 17.2 %copy-start.2 = (bf16[1024,256]{1,0:T(8,128)(2,1)S(1)}, bf16[1024,256]{1,0:T(8,128)(2,1)}, u32[]{:S(2)}) copy-start(bf16[1024,256]{1,0:T(8,128)(2,1)} %param.15) | copy-start | bytes 1572868
  35.1 17.2 %copy-start.3 = (bf16[1024,256]{1,0:T(8,128)(2,1)S(1)}, bf16[1024,256]{1,0:T(8,128)(2,1)}, u32[]{:S(2)}) copy-start(bf16[1024,256]{1,0:T(8,128)(2,1)} %param.14) | copy-start | bytes 1572868
  79.6 7.4 %all-to-all-start.3 = ((f32[4,2,512]{2,1,0:T(2,128)}), f32[4,2,512]{2,1,0:T(2,128)S(1)}, u32[]{:S(2)}, u32[]{:S(2)}) async-start(f32[4,2,512]{2,1,0:T(2,128)} %broadcast_in_dim.8), calls=%async_computation.3 | async-start | bytes 32768 | tf_op jit(solution)/shard_map/all_to_all | solution.py:30

commit v6 on v5

--- a/solution.py
+++ b/solution.py
@@ -34,23 +34,28 @@
 HEAD = 64
 
 
-def attend_kernel(lens_ref, q_ref, kn_ref, vn_ref, kc_ref, vc_ref, out_ref):
+def attend_kernel(lens_ref, rows_ref, wj_ref, kc_ref, vc_ref, wo_ref, out_ref):
     g = pl.program_id(0)
     length = lens_ref[g]
-    new_count = q_ref.shape[1]
+    new_count = rows_ref.shape[1]
     span = kc_ref.shape[1]
-    heads = q_ref.shape[2] // HEAD
+    width = kc_ref.shape[2]
+    heads = width // HEAD
+    qkv = jnp.dot(rows_ref[0], wj_ref[...], preferred_element_type=jnp.float32).astype(jnp.bfloat16)
     cache_pos = lax.broadcasted_iota(jnp.int32, (new_count, span), 1)
     cache_ok = cache_pos < length
     row = lax.broadcasted_iota(jnp.int32, (new_count, new_count), 0)
     col = lax.broadcasted_iota(jnp.int32, (new_count, new_count), 1)
     new_ok = col <= row
     dims = (((1,), (1,)), ((), ()))
+    parts = []
     for h in range(heads):
         cols = slice(h * HEAD, (h + 1) * HEAD)
-        qh = q_ref[0, :, cols]
+        qh = qkv[:, h * HEAD:(h + 1) * HEAD]
+        kn = qkv[:, width + h * HEAD:width + (h + 1) * HEAD]
+        vn = qkv[:, 2 * width + h * HEAD:2 * width + (h + 1) * HEAD]
         sc = lax.dot_general(qh, kc_ref[0, :, cols], dims, preferred_element_type=jnp.float32) * HEAD ** (-0.5)
-        sn = lax.dot_general(qh, kn_ref[0, :, cols], dims, preferred_element_type=jnp.float32) * HEAD ** (-0.5)
+        sn = lax.dot_general(qh, kn, dims, preferred_element_type=jnp.float32) * HEAD ** (-0.5)
         sc = jnp.where(cache_ok, sc, -jnp.inf)
         sn = jnp.where(new_ok, sn, -jnp.inf)
         top = jnp.maximum(jnp.max(sc, axis=1, keepdims=True), jnp.max(sn, axis=1, keepdims=True))
@@ -58,28 +63,33 @@
         wn = jnp.exp(sn - top)
         total = jnp.sum(wc, axis=1, keepdims=True) + jnp.sum(wn, axis=1, keepdims=True)
         ctx = jnp.dot(wc.astype(jnp.bfloat16), vc_ref[0, :, cols], preferred_element_type=jnp.float32)
-        ctx = ctx + jnp.dot(wn.astype(jnp.bfloat16), vn_ref[0, :, cols], preferred_element_type=jnp.float32)
-        out_ref[0, :, cols] = (ctx / total).astype(out_ref.dtype)
-
-
-def attend_pallas(queries, new_keys, new_values, k_cache, v_cache, cache_len):
+        ctx = ctx + jnp.dot(wn.astype(jnp.bfloat16), vn, preferred_element_type=jnp.float32)
+        parts.append((ctx / total).astype(jnp.bfloat16))
+    context = jnp.concatenate(parts, axis=1)
+    out_ref[0] = jnp.dot(context, wo_ref[...], preferred_element_type=jnp.float32).astype(out_ref.dtype)
+
+
+def attend_pallas(whole, w_joined, k_cache, v_cache, w_out, cache_len):
     requests, span, width = k_cache.shape
-    new_count = queries.shape[0] // requests
-    shape3 = (requests, new_count, width)
-    q3, kn3, vn3 = (a.reshape(shape3) for a in (queries, new_keys, new_values))
-    new_spec = pl.BlockSpec((1, new_count, width), lambda g, lens: (g, 0, 0))
+    new_count = whole.shape[0] // requests
+    feats = whole.shape[1]
+    rows = whole.reshape(requests, new_count, feats)
+    row_spec = pl.BlockSpec((1, new_count, feats), lambda g, lens: (g, 0, 0))
     cache_spec = pl.BlockSpec((1, span, width), lambda g, lens: (g, 0, 0))
+    wj_spec = pl.BlockSpec(w_joined.shape, lambda g, lens: (0, 0))
+    wo_spec = pl.BlockSpec(w_out.shape, lambda g, lens: (0, 0))
+    out_spec = pl.BlockSpec((1, new_count, w_out.shape[1]), lambda g, lens: (g, 0, 0))
     out = pl.pallas_call(
         attend_kernel,
-        out_shape=jax.ShapeDtypeStruct(shape3, jnp.bfloat16),
+        out_shape=jax.ShapeDtypeStruct((requests, new_count, w_out.shape[1]), jnp.bfloat16),
         grid_spec=pltpu.PrefetchScalarGridSpec(
             num_scalar_prefetch=1,
             grid=(requests,),
-            in_specs=[new_spec, new_spec, new_spec, cache_spec, cache_spec],
-            out_specs=new_spec,
+            in_specs=[row_spec, wj_spec, cache_spec, cache_spec, wo_spec],
+            out_specs=out_spec,
         ),
-    )(cache_len, q3, kn3, vn3, k_cache, v_cache)
-    return out.reshape(queries.shape)
+    )(cache_len, rows, w_joined, k_cache, v_cache, w_out)
+    return out.reshape(whole.shape[0], w_out.shape[1])
 
 
 def head_view(array, head_size):
@@ -135,10 +145,9 @@
     return (all_three[:, :width], all_three[:, width:2 * width], all_three[:, 2 * width:])
 
 
-def finish_rows(context, local, w_out, ln_gain, ln_bias):
+def finish_rows(partial_sum, local, ln_gain, ln_bias):
     row_count, feat_width = local.shape
-    partial_sum = jnp.dot(context, w_out, preferred_element_type=jnp.float32)
-    attended = scatter_sum_tp(partial_sum.astype(jnp.bfloat16))
+    attended = scatter_sum_tp(partial_sum)
     summed = local.astype(jnp.float32) + attended
     first_sum, square_sum = sum_tp(
         jnp.stack([jnp.sum(summed, axis=1), jnp.sum(summed * summed, axis=1)])
@@ -174,9 +183,9 @@
         ordered, "req", split_axis=0, concat_axis=0, tiled=True
     ).reshape(row_count, feat_width)
     whole = gather_tp(arrived)
-    queries, new_keys, new_values = project_rows(whole, w_query, w_key, w_value)
-    context = attend_pallas(queries, new_keys, new_values, k_cache, v_cache, cache_len)
-    normed = finish_rows(context, arrived, w_out, ln_gain, ln_bias)
+    w_joined = jnp.concatenate([w_query, w_key, w_value], 1)
+    partial_sum = attend_pallas(whole, w_joined, k_cache, v_cache, w_out, cache_len)
+    normed = finish_rows(partial_sum, arrived, ln_gain, ln_bias)
     returned = lax.all_to_all(to_blocks(normed), "req", split_axis=0, concat_axis=0, tiled=True)
     back = jnp.einsum("ja,jif->aif", choose, returned, preferred_element_type=jnp.float32)
     return back.astype(jnp.bfloat16).reshape(row_count, feat_width)

time: 115 us -> 120 us (1.043)
  blocking collectives: 89.9 us -> 73 us
  waiting for transfers between devices: 2.65 us -> 14.6 us
  local copies, waits for them, and re-layouts: 6.16 us -> 10.4 us
  starting transfers between devices: 3.25 us -> 7.27 us
  Pallas kernels: 7.78 us -> 10.8 us
  matrix products: 3.02 us -> 0.6 us
  other arithmetic: 1.7 us -> 2.9 us
    all_to_all x1 -> x0, blocking collectives: 17.2 us -> none  [gather_tp(): got = lax.all_to_all(copies, 'tp', 0, 0, tiled=True)]
    all_to_all x0 -> x1, waiting for transfers between devices: none -> 12 us  [gather_tp(): got = lax.all_to_all(copies, 'tp', 0, 0, tiled=True)]
    all_to_all x0 -> x1, starting transfers between devices: none -> 4.01 us  [gather_tp(): got = lax.all_to_all(copies, 'tp', 0, 0, tiled=True)]
    another operation x0 -> x3, local copies, waits for them, and re-layouts: none -> 3.54 us  [the longest x2 1.99 us: scatter_sum_tp(): pieces = jnp.moveaxis(whole.reshape(rows, count, width // count), 1, 0)]
    pallas_call x1, Pallas kernels: 7.78 us -> 10.8 us  [attend_pallas(): pl.pallas_call(attend_kernel, out_shape=jax.ShapeDtypeStruct((requests, n...]
    dot_general x2 -> x0, matrix products: 2.43 us -> none  [the longest x1 1.39 us: finish_rows(): partial_sum = jnp.dot(context, w_out, preferred_element_type=jnp.float32)]
    concatenate x0 -> x1, other arithmetic: none -> 1.26 us  [shards(): w_joined = jnp.concatenate([w_query, w_key, w_value], 1)]
  transfers between devices with their start and end apart: 1 -> 2, of which waited for: 1 -> 2; matrix products, arithmetic and copies ran while one was open for 1% -> 2% of each run, Pallas kernels for 0% -> 0%
where the time goes in v6:
time: 120 us
  blocking collectives  73 us (61%)
  waiting for transfers between devices  14.6 us (12%)
  Pallas kernels  10.8 us (9%)
  local copies, waits for them, and re-layouts  10.4 us (9%)
  starting transfers between devices  7.27 us (6%)
  other arithmetic  2.9 us (2%)
    all_to_all x1, blocking collectives, shards(): lax.all_to_all(ordered, 'req', split_axis=0, concat_axis=0, tiled=True)  32.5 us
    all_to_all x1, blocking collectives, shards(): lax.all_to_all(to_blocks(normed), 'req', split_axis=0, concat_axis=0, til...  26 us
    all_to_all x1, blocking collectives, scatter_sum_tp(): got = lax.all_to_all(pieces, 'tp', 0, 0, tiled=True)  14.5 us
    all_to_all x1, waiting for transfers between devices, gather_tp(): got = lax.all_to_all(copies, 'tp', 0, 0, tiled=True)  12 us
    pallas_call x1, Pallas kernels, attend_pallas(): pl.pallas_call(attend_kernel, out_shape=jax.ShapeDtypeStruct((requests, n...  10.8 us
    all_to_all x1, starting transfers between devices, gather_tp(): got = lax.all_to_all(copies, 'tp', 0, 0, tiled=True)  4.01 us
    all_to_all x1, starting transfers between devices, sum_tp(): got = lax.all_to_all(copies, 'tp', 0, 0, tiled=True)  3.25 us
    all_to_all x1, waiting for transfers between devices, sum_tp(): got = lax.all_to_all(copies, 'tp', 0, 0, tiled=True)  2.65 us
  transfers between devices with their start and end apart: 2, of which 2 were waited for; matrix products, arithmetic and copies ran while one was open for 2% of the time, Pallas kernels for 0%

profile of v6, /device:TPU:1, one launch (start us, length us, event | category | flops | bytes accessed | tf_op | source)
XLA Modules:
  0.0 119.8 jit_solution(1633872842330169287)
XLA Ops:
  0.0 0.7 and_select_fusion
  0.7 1.0 reshape.63
  1.7 0.3 convolution_convert_fusion.1
  2.0 0.2 copy.45
  2.2 32.5 %all_to_all.25 = bf16[128,4,256]{2,1,0:T(4,128)(2,1)S(1)} all-to-all(bf16[128,4,256]{2,1,0:T(4,128)(2,1)S(1)} %copy.45), channel_id=1, replica_groups=mesh['req'=128,'tp'=4] {'req'}, dimensions={0} | all-to-all | bytes 524288 | tf_op jit(solution)/shard_map/all_to_all | solution.py:182
  34.9 1.0 broadcast_in_dim.7
  35.9 4.0 %all-to-all-start.1 = ((bf16[4,512,256]{2,1,0:T(8,128)(2,1)}), bf16[4,512,256]{2,1,0:T(8,128)(2,1)S(1)}, u32[]{:S(2)}, u32[]{:S(2)}) async-start(bf16[4,512,256]{2,1,0:T(8,128)(2,1)} %broadcast_in_dim.7), calls=%async_computation.1 | async-start | bytes 2097152 | tf_op jit(solution)/shard_map/all_to_all | solution.py:15
  39.9 1.3 %pad_maximum_fusion.wj_ref = bf16[1024,768]{1,0:T(8,128)(2,1)} fusion(bf16[1024,256]{1,0:T(8,128)(2,1)S(1)} %copy-done, bf16[1024,256]{1,0:T(8,128)(2,1)S(1)} %copy-done.1, bf16[1024,256]{1,0:T(8,128)(2,1)S(1)} %copy-done.2), kind=kLoop, calls=%fused_computation.1 | loop fusion | flops 4718592 | bytes 3145728 | tf_op jit(solution)/shard_map/concatenate | solution.py:186
  41.2 12.0 %all-to-all-done.1 = bf16[4,512,256]{2,1,0:T(8,128)(2,1)S(1)} async-done(((bf16[4,512,256]{2,1,0:T(8,128)(2,1)}), bf16[4,512,256]{2,1,0:T(8,128)(2,1)S(1)}, u32[]{:S(2)}, u32[]{:S(2)}) %all-to-all-start.1) | async-done | bytes 1048608 | tf_op jit(solution)/shard_map/all_to_all | solution.py:15
  53.1 0.8 copy.46
  54.0 1.6 %reshape_reshape.6.rows_ref = bf16[2,256,1024]{2,1,0:T(8,128)(2,1)} reshape(bf16[512,4,256]{2,1,0:T(4,128)(2,1)S(1)} %copy.46) | data formatting | bytes 2097152 | tf_op jit(solution)/shard_map/reshape;reshape | solution.py:76
  55.5 10.8 %shard_map.109 = bf16[2,256,1024]{2,1,0:T(8,128)(2,1)} custom-call(s32[2]{0:T(128)} %lens_ref.1, bf16[2,256,1024]{2,1,0:T(8,128)(2,1)} %reshape_reshape.6.rows_ref, bf16[1024,768]{1,0:T(8,128)(2,1)} %pad_maximum_fusion.wj_ref, bf16[2,1024,256]{2,1,0:T(8,128)(2,1)} %kc_ref.1, bf16[2,1024,256]{2,1,0:T(8,128)(2,1)} %vc_ref.1, bf16[256,1024]{1,0:T(8,128)(2,1)} %wo_ref.1), custom_call_target="tpu_custom_call" | custom-call | tf_op jit(solution)/shard_map/pallas_call | solution.py:82
  66.3 1.9 %reshape_reshape.7 = bf16[512,4,256]{2,1,0:T(4,128)(2,1)S(1)} reshape(bf16[2,256,1024]{2,1,0:T(8,128)(2,1)} %shard_map.109) | data formatting | bytes 2097152 | tf_op jit(solution)/shard_map/reshape;reshape | solution.py:22
  68.3 14.5 %all_to_all.26 = bf16[4,512,256]{2,1,0:T(8,128)(2,1)S(1)} all-to-all(bf16[4,512,256]{2,1,0:T(8,128)(2,1)S(1)} %bitcast.10), channel_id=1, replica_groups=mesh['req'=128,'tp'=4] {'tp'}, dimensions={0} | all-to-all | bytes 2097152 | tf_op jit(solution)/shard_map/all_to_all | solution.py:23
  83.2 0.4 fusion.2
  83.8 0.6 broadcast_in_dim.8
  84.4 3.3 %all-to-all-start.3 = ((f32[4,2,512]{2,1,0:T(2,128)}), f32[4,2,512]{2,1,0:T(2,128)S(1)}, u32[]{:S(2)}, u32[]{:S(2)}) async-start(f32[4,2,512]{2,1,0:T(2,128)} %broadcast_in_dim.8), calls=%async_computation.3 | async-start | bytes 32768 | tf_op jit(solution)/shard_map/all_to_all | solution.py:30
  87.7 0.8 dynamic_slice.6
  88.5 0.8 dynamic_slice.7
  89.2 2.6 %all-to-all-done.3 = f32[4,2,512]{2,1,0:T(2,128)S(1)} async-done(((f32[4,2,512]{2,1,0:T(2,128)}), f32[4,2,512]{2,1,0:T(2,128)S(1)}, u32[]{:S(2)}, u32[]{:S(2)}) %all-to-all-start.3) | async-done | bytes 16416 | tf_op jit(solution)/shard_map/all_to_all | solution.py:30
  92.2 0.4 add_convert_fusion
  92.5 26.0 %all_to_all.27 = bf16[128,4,256]{2,1,0:T(4,128)(2,1)S(1)} all-to-all(bf16[128,4,256]{2,1,0:T(4,128)(2,1)S(1)} %add_convert_fusion), channel_id=1, replica_groups=mesh['req'=128,'tp'=4] {'req'}, dimensions={0} | all-to-all | bytes 524288 | tf_op jit(solution)/shard_map/all_to_all | solution.py:189
  118.5 0.3 convolution_convert_fusion
  119.0 0.8 reshape.64
  (19 shorter events, 1.2 us)
Async XLA Ops:
  34.8 5.1 %copy-start = (bf16[1024,256]{1,0:T(8,128)(2,1)S(1)}, bf16[1024,256]{1,0:T(8,128)(2,1)}, u32[]{:S(2)}) copy-start(bf16[1024,256]{1,0:T(8,128)(2,1)} %param.16) | copy-start | bytes 1572868
  34.8 5.1 %copy-start.1 = (bf16[1024,256]{1,0:T(8,128)(2,1)S(1)}, bf16[1024,256]{1,0:T(8,128)(2,1)}, u32[]{:S(2)}) copy-start(bf16[1024,256]{1,0:T(8,128)(2,1)} %param.15) | copy-start | bytes 1572868
  34.8 5.1 %copy-start.2 = (bf16[1024,256]{1,0:T(8,128)(2,1)S(1)}, bf16[1024,256]{1,0:T(8,128)(2,1)}, u32[]{:S(2)}) copy-start(bf16[1024,256]{1,0:T(8,128)(2,1)} %param.14) | copy-start | bytes 1572868
  35.9 17.3 %all-to-all-start.1 = ((bf16[4,512,256]{2,1,0:T(8,128)(2,1)}), bf16[4,512,256]{2,1,0:T(8,128)(2,1)S(1)}, u32[]{:S(2)}, u32[]{:S(2)}) async-start(bf16[4,512,256]{2,1,0:T(8,128)(2,1)} %broadcast_in_dim.7), calls=%async_computation.1 | async-start | bytes 2097152 | tf_op jit(solution)/shard_map/all_to_all | solution.py:15
  84.4 7.4 %all-to-all-start.3 = ((f32[4,2,512]{2,1,0:T(2,128)}), f32[4,2,512]{2,1,0:T(2,128)S(1)}, u32[]{:S(2)}, u32[]{:S(2)}) async-start(f32[4,2,512]{2,1,0:T(2,128)} %broadcast_in_dim.8), calls=%async_computation.3 | async-start | bytes 32768 | tf_op jit(solution)/shard_map/all_to_all | solution.py:30

commit v7 on v5

--- a/solution.py
+++ b/solution.py
@@ -34,7 +34,7 @@
 HEAD = 64
 
 
-def attend_kernel(lens_ref, q_ref, kn_ref, vn_ref, kc_ref, vc_ref, out_ref):
+def attend_kernel(lens_ref, q_ref, kn_ref, vn_ref, kc_ref, vc_ref, wo_ref, out_ref):
     g = pl.program_id(0)
     length = lens_ref[g]
     new_count = q_ref.shape[1]
@@ -46,6 +46,7 @@
     col = lax.broadcasted_iota(jnp.int32, (new_count, new_count), 1)
     new_ok = col <= row
     dims = (((1,), (1,)), ((), ()))
+    parts = []
     for h in range(heads):
         cols = slice(h * HEAD, (h + 1) * HEAD)
         qh = q_ref[0, :, cols]
@@ -59,10 +60,12 @@
         total = jnp.sum(wc, axis=1, keepdims=True) + jnp.sum(wn, axis=1, keepdims=True)
         ctx = jnp.dot(wc.astype(jnp.bfloat16), vc_ref[0, :, cols], preferred_element_type=jnp.float32)
         ctx = ctx + jnp.dot(wn.astype(jnp.bfloat16), vn_ref[0, :, cols], preferred_element_type=jnp.float32)
-        out_ref[0, :, cols] = (ctx / total).astype(out_ref.dtype)
-
-
-def attend_pallas(queries, new_keys, new_values, k_cache, v_cache, cache_len):
+        parts.append((ctx / total).astype(jnp.bfloat16))
+    context = jnp.concatenate(parts, axis=1)
+    out_ref[0] = jnp.dot(context, wo_ref[...], preferred_element_type=jnp.float32).astype(out_ref.dtype)
+
+
+def attend_pallas(queries, new_keys, new_values, k_cache, v_cache, w_out, cache_len):
     requests, span, width = k_cache.shape
     new_count = queries.shape[0] // requests
     shape3 = (requests, new_count, width)
@@ -71,15 +74,16 @@
     cache_spec = pl.BlockSpec((1, span, width), lambda g, lens: (g, 0, 0))
     out = pl.pallas_call(
         attend_kernel,
-        out_shape=jax.ShapeDtypeStruct(shape3, jnp.bfloat16),
+        out_shape=jax.ShapeDtypeStruct((requests, new_count, w_out.shape[1]), jnp.bfloat16),
         grid_spec=pltpu.PrefetchScalarGridSpec(
             num_scalar_prefetch=1,
             grid=(requests,),
-            in_specs=[new_spec, new_spec, new_spec, cache_spec, cache_spec],
-            out_specs=new_spec,
+            in_specs=[new_spec, new_spec, new_spec, cache_spec, cache_spec,
+                      pl.BlockSpec(w_out.shape, lambda g, lens: (0, 0))],
+            out_specs=pl.BlockSpec((1, new_count, w_out.shape[1]), lambda g, lens: (g, 0, 0)),
         ),
-    )(cache_len, q3, kn3, vn3, k_cache, v_cache)
-    return out.reshape(queries.shape)
+    )(cache_len, q3, kn3, vn3, k_cache, v_cache, w_out)
+    return out.reshape(queries.shape[0], w_out.shape[1])
 
 
 def head_view(array, head_size):
@@ -135,10 +139,9 @@
     return (all_three[:, :width], all_three[:, width:2 * width], all_three[:, 2 * width:])
 
 
-def finish_rows(context, local, w_out, ln_gain, ln_bias):
+def finish_rows(partial_sum, local, ln_gain, ln_bias):
     row_count, feat_width = local.shape
-    partial_sum = jnp.dot(context, w_out, preferred_element_type=jnp.float32)
-    attended = scatter_sum_tp(partial_sum.astype(jnp.bfloat16))
+    attended = scatter_sum_tp(partial_sum)
     summed = local.astype(jnp.float32) + attended
     first_sum, square_sum = sum_tp(
         jnp.stack([jnp.sum(summed, axis=1), jnp.sum(summed * summed, axis=1)])
@@ -175,8 +178,8 @@
     ).reshape(row_count, feat_width)
     whole = gather_tp(arrived)
     queries, new_keys, new_values = project_rows(whole, w_query, w_key, w_value)
-    context = attend_pallas(queries, new_keys, new_values, k_cache, v_cache, cache_len)
-    normed = finish_rows(context, arrived, w_out, ln_gain, ln_bias)
+    partial_sum = attend_pallas(queries, new_keys, new_values, k_cache, v_cache, w_out, cache_len)
+    normed = finish_rows(partial_sum, arrived, ln_gain, ln_bias)
     returned = lax.all_to_all(to_blocks(normed), "req", split_axis=0, concat_axis=0, tiled=True)
     back = jnp.einsum("ja,jif->aif", choose, returned, preferred_element_type=jnp.float32)
     return back.astype(jnp.bfloat16).reshape(row_count, feat_width)

time: 115 us -> 117 us (1.017)
  local copies, waits for them, and re-layouts: 6.16 us -> 8.1 us
  Pallas kernels: 7.78 us -> 9.6 us
  matrix products: 3.02 us -> 1.64 us
    another operation x0 -> x2, local copies, waits for them, and re-layouts: none -> 1.99 us  [scatter_sum_tp(): pieces = jnp.moveaxis(whole.reshape(rows, count, width // count), 1, 0)]
    pallas_call x1, Pallas kernels: 7.78 us -> 9.6 us  [attend_pallas(): pl.pallas_call(attend_kernel, out_shape=jax.ShapeDtypeStruct((requests, n...]
    dot_general x1 -> x0, matrix products: 1.39 us -> none  [finish_rows(): partial_sum = jnp.dot(context, w_out, preferred_element_type=jnp.float32)]
where the time goes in v7:
time: 117 us
  blocking collectives  89.9 us (77%)
  Pallas kernels  9.6 us (8%)
  local copies, waits for them, and re-layouts  8.1 us (7%)
  starting transfers between devices  3.25 us (3%)
  waiting for transfers between devices  2.65 us (2%)
  other arithmetic  1.64 us (1%)
  matrix products  1.64 us (1%)
    all_to_all x1, blocking collectives, shards(): lax.all_to_all(ordered, 'req', split_axis=0, concat_axis=0, tiled=True)  32.5 us
    all_to_all x1, blocking collectives, shards(): lax.all_to_all(to_blocks(normed), 'req', split_axis=0, concat_axis=0, til...  25.7 us
    all_to_all x1, blocking collectives, gather_tp(): got = lax.all_to_all(copies, 'tp', 0, 0, tiled=True)  17.2 us
    all_to_all x1, blocking collectives, scatter_sum_tp(): got = lax.all_to_all(pieces, 'tp', 0, 0, tiled=True)  14.5 us
    pallas_call x1, Pallas kernels, attend_pallas(): pl.pallas_call(attend_kernel, out_shape=jax.ShapeDtypeStruct((requests, n...  9.6 us
    all_to_all x1, starting transfers between devices, sum_tp(): got = lax.all_to_all(copies, 'tp', 0, 0, tiled=True)  3.25 us
    all_to_all x1, waiting for transfers between devices, sum_tp(): got = lax.all_to_all(copies, 'tp', 0, 0, tiled=True)  2.65 us
  transfers between devices with their start and end apart: 1, of which 1 were waited for; matrix products, arithmetic and copies ran while one was open for 1% of the time, Pallas kernels for 0%

profile of v7, /device:TPU:1, one launch (start us, length us, event | category | flops | bytes accessed | tf_op | source)
XLA Modules:
  0.0 117.0 jit_solution(12714190730652381797)
XLA Ops:
  0.0 0.7 and_select_fusion
  0.7 1.0 reshape.75
  1.7 0.3 convolution_convert_fusion.1
  2.0 0.2 copy.46
  2.2 32.5 %all_to_all.25 = bf16[128,4,256]{2,1,0:T(4,128)(2,1)S(1)} all-to-all(bf16[128,4,256]{2,1,0:T(4,128)(2,1)S(1)} %copy.46), channel_id=1, replica_groups=mesh['req'=128,'tp'=4] {'req'}, dimensions={0} | all-to-all | bytes 524288 | tf_op jit(solution)/shard_map/all_to_all | solution.py:176
  35.1 17.2 %all_to_all.26 = bf16[4,512,256]{1,2,0:T(8,128)(2,1)S(1)} all-to-all(bf16[4,512,256]{1,2,0:T(8,128)(2,1)S(1)} %broadcast_in_dim.7), channel_id=1, replica_groups=mesh['req'=128,'tp'=4] {'tp'}, dimensions={0} | all-to-all | bytes 2097152 | tf_op jit(solution)/shard_map/all_to_all | solution.py:15
  52.3 1.0 fusion.6
  53.3 0.9 fusion.20
  54.2 9.6 %shard_map.109 = bf16[2,256,1024]{2,1,0:T(8,128)(2,1)} custom-call(s32[2]{0:T(128)} %lens_ref.1, bf16[2,256,256]{2,1,0:T(8,128)(2,1)} %bitcast.19, bf16[2,256,256]{2,1,0:T(8,128)(2,1)} %bitcast.18, bf16[2,256,256]{2,1,0:T(8,128)(2,1)} %bitcast.17, bf16[2,1024,256]{2,1,0:T(8,128)(2,1)} %kc_ref.1, bf16[2,1024,256]{2,1,0:T(8,128)(2,1)} %vc_ref.1, ...), custom_call_target="tpu_custom_call" | custom-call | tf_op jit(solution)/shard_map/pallas_call | solution.py:75
  63.8 1.9 %reshape_reshape.3 = bf16[512,4,256]{2,1,0:T(4,128)(2,1)S(1)} reshape(bf16[2,256,1024]{2,1,0:T(8,128)(2,1)} %shard_map.109) | data formatting | bytes 2097152 | tf_op jit(solution)/shard_map/reshape;reshape | solution.py:22
  65.9 14.5 %all_to_all.27 = bf16[4,512,256]{2,1,0:T(8,128)(2,1)S(1)} all-to-all(bf16[4,512,256]{2,1,0:T(8,128)(2,1)S(1)} %bitcast.15), channel_id=1, replica_groups=mesh['req'=128,'tp'=4] {'tp'}, dimensions={0} | all-to-all | bytes 2097152 | tf_op jit(solution)/shard_map/all_to_all | solution.py:23
  80.4 0.1 convert_reduce_fusion
  80.5 0.1 reduce_sum.39
  80.7 0.4 fusion.11
  81.3 0.6 broadcast_in_dim.8
  81.9 3.3 %all-to-all-start.3 = ((f32[4,2,512]{2,1,0:T(2,128)}), f32[4,2,512]{2,1,0:T(2,128)S(1)}, u32[]{:S(2)}, u32[]{:S(2)}) async-start(f32[4,2,512]{2,1,0:T(2,128)} %broadcast_in_dim.8), calls=%async_computation.3 | async-start | bytes 32768 | tf_op jit(solution)/shard_map/all_to_all | solution.py:30
  85.2 0.8 dynamic_slice.6
  85.9 0.8 dynamic_slice.7
  86.7 2.6 %all-to-all-done.3 = f32[4,2,512]{2,1,0:T(2,128)S(1)} async-done(((f32[4,2,512]{2,1,0:T(2,128)}), f32[4,2,512]{2,1,0:T(2,128)S(1)}, u32[]{:S(2)}, u32[]{:S(2)}) %all-to-all-start.3) | async-done | bytes 16416 | tf_op jit(solution)/shard_map/all_to_all | solution.py:30
  89.6 0.4 add_convert_fusion
  90.0 25.7 %all_to_all.28 = bf16[128,4,256]{2,1,0:T(4,128)(2,1)S(1)} all-to-all(bf16[128,4,256]{2,1,0:T(4,128)(2,1)S(1)} %add_convert_fusion), channel_id=1, replica_groups=mesh['req'=128,'tp'=4] {'req'}, dimensions={0} | all-to-all | bytes 524288 | tf_op jit(solution)/shard_map/all_to_all | solution.py:183
  115.7 0.3 convolution_convert_fusion
  116.0 0.2 copy.55
  116.2 0.8 reshape.80
  (18 shorter events, 0.9 us)
Async XLA Ops:
  35.1 17.2 %copy-start = (bf16[1024,256]{1,0:T(8,128)(2,1)S(1)}, bf16[1024,256]{1,0:T(8,128)(2,1)}, u32[]{:S(2)}) copy-start(bf16[1024,256]{1,0:T(8,128)(2,1)} %param.16) | copy-start | bytes 1572868
  35.1 17.2 %copy-start.1 = (bf16[1024,256]{1,0:T(8,128)(2,1)S(1)}, bf16[1024,256]{1,0:T(8,128)(2,1)}, u32[]{:S(2)}) copy-start(bf16[1024,256]{1,0:T(8,128)(2,1)} %param.15) | copy-start | bytes 1572868
  35.1 17.2 %copy-start.2 = (bf16[1024,256]{1,0:T(8,128)(2,1)S(1)}, bf16[1024,256]{1,0:T(8,128)(2,1)}, u32[]{:S(2)}) copy-start(bf16[1024,256]{1,0:T(8,128)(2,1)} %param.14) | copy-start | bytes 1572868
  81.9 7.4 %all-to-all-start.3 = ((f32[4,2,512]{2,1,0:T(2,128)}), f32[4,2,512]{2,1,0:T(2,128)S(1)}, u32[]{:S(2)}, u32[]{:S(2)}) async-start(f32[4,2,512]{2,1,0:T(2,128)} %broadcast_in_dim.8), calls=%async_computation.3 | async-start | bytes 32768 | tf_op jit(solution)/shard_map/all_to_all | solution.py:30

commit v8 on v5

--- a/solution.py
+++ b/solution.py
@@ -62,24 +62,26 @@
         out_ref[0, :, cols] = (ctx / total).astype(out_ref.dtype)
 
 
-def attend_pallas(queries, new_keys, new_values, k_cache, v_cache, cache_len):
+def attend_pallas(joined, k_cache, v_cache, cache_len):
     requests, span, width = k_cache.shape
-    new_count = queries.shape[0] // requests
-    shape3 = (requests, new_count, width)
-    q3, kn3, vn3 = (a.reshape(shape3) for a in (queries, new_keys, new_values))
-    new_spec = pl.BlockSpec((1, new_count, width), lambda g, lens: (g, 0, 0))
+    new_count = joined.shape[0] // requests
+    packed = joined.reshape(requests, new_count, joined.shape[1])
+
+    def new_spec(part):
+        return pl.BlockSpec((1, new_count, width), lambda g, lens: (g, 0, part))
+
     cache_spec = pl.BlockSpec((1, span, width), lambda g, lens: (g, 0, 0))
     out = pl.pallas_call(
         attend_kernel,
-        out_shape=jax.ShapeDtypeStruct(shape3, jnp.bfloat16),
+        out_shape=jax.ShapeDtypeStruct((requests, new_count, width), jnp.bfloat16),
         grid_spec=pltpu.PrefetchScalarGridSpec(
             num_scalar_prefetch=1,
             grid=(requests,),
-            in_specs=[new_spec, new_spec, new_spec, cache_spec, cache_spec],
-            out_specs=new_spec,
+            in_specs=[new_spec(0), new_spec(1), new_spec(2), cache_spec, cache_spec],
+            out_specs=new_spec(0),
         ),
-    )(cache_len, q3, kn3, vn3, k_cache, v_cache)
-    return out.reshape(queries.shape)
+    )(cache_len, packed, packed, packed, k_cache, v_cache)
+    return out.reshape(joined.shape[0], width)
 
 
 def head_view(array, head_size):
@@ -132,7 +134,7 @@
     width = w_query.shape[1]
     joined = jnp.concatenate([w_query, w_key, w_value], 1)
     all_three = jnp.dot(whole, joined, preferred_element_type=jnp.float32).astype(jnp.bfloat16)
-    return (all_three[:, :width], all_three[:, width:2 * width], all_three[:, 2 * width:])
+    return all_three
 
 
 def finish_rows(context, local, w_out, ln_gain, ln_bias):
@@ -174,8 +176,8 @@
         ordered, "req", split_axis=0, concat_axis=0, tiled=True
     ).reshape(row_count, feat_width)
     whole = gather_tp(arrived)
-    queries, new_keys, new_values = project_rows(whole, w_query, w_key, w_value)
-    context = attend_pallas(queries, new_keys, new_values, k_cache, v_cache, cache_len)
+    joined = project_rows(whole, w_query, w_key, w_value)
+    context = attend_pallas(joined, k_cache, v_cache, cache_len)
     normed = finish_rows(context, arrived, w_out, ln_gain, ln_bias)
     returned = lax.all_to_all(to_blocks(normed), "req", split_axis=0, concat_axis=0, tiled=True)
     back = jnp.einsum("ja,jif->aif", choose, returned, preferred_element_type=jnp.float32)

time: 115 us -> 115 us (level)
  no operation moved by 1% of the time
where the time goes in v8:
time: 115 us
  blocking collectives  89.9 us (78%)
  Pallas kernels  7.81 us (7%)
  local copies, waits for them, and re-layouts  5.27 us (5%)
  matrix products  3.9 us (3%)
  starting transfers between devices  3.25 us (3%)
  waiting for transfers between devices  2.65 us (2%)
  other arithmetic  1.7 us (1%)
    all_to_all x1, blocking collectives, shards(): lax.all_to_all(ordered, 'req', split_axis=0, concat_axis=0, tiled=True)  32.5 us
    all_to_all x1, blocking collectives, shards(): lax.all_to_all(to_blocks(normed), 'req', split_axis=0, concat_axis=0, til...  25.7 us
    all_to_all x1, blocking collectives, gather_tp(): got = lax.all_to_all(copies, 'tp', 0, 0, tiled=True)  17.2 us
    all_to_all x1, blocking collectives, scatter_sum_tp(): got = lax.all_to_all(pieces, 'tp', 0, 0, tiled=True)  14.5 us
    pallas_call x1, Pallas kernels, attend_pallas(): pl.pallas_call(attend_kernel, out_shape=jax.ShapeDtypeStruct((requests, n...  7.81 us
    all_to_all x1, starting transfers between devices, sum_tp(): got = lax.all_to_all(copies, 'tp', 0, 0, tiled=True)  3.25 us
    all_to_all x1, waiting for transfers between devices, sum_tp(): got = lax.all_to_all(copies, 'tp', 0, 0, tiled=True)  2.65 us
  transfers between devices with their start and end apart: 1, of which 1 were waited for; matrix products, arithmetic and copies ran while one was open for 1% of the time, Pallas kernels for 0%

profile of v8, /device:TPU:1, one launch (start us, length us, event | category | flops | bytes accessed | tf_op | source)
XLA Modules:
  0.0 114.7 jit_solution(8935100556504940095)
XLA Ops:
  0.0 0.7 and_select_fusion
  0.7 1.0 reshape.75
  1.7 0.3 convolution_convert_fusion.2
  2.1 0.2 copy.46
  2.3 32.5 %all_to_all.25 = bf16[128,4,256]{2,1,0:T(4,128)(2,1)S(1)} all-to-all(bf16[128,4,256]{2,1,0:T(4,128)(2,1)S(1)} %copy.46), channel_id=1, replica_groups=mesh['req'=128,'tp'=4] {'req'}, dimensions={0} | all-to-all | bytes 524288 | tf_op jit(solution)/shard_map/all_to_all | solution.py:175
  34.9 0.1 copy.47
  35.2 17.2 %all_to_all.26 = bf16[4,512,256]{1,2,0:T(8,128)(2,1)S(1)} all-to-all(bf16[4,512,256]{1,2,0:T(8,128)(2,1)S(1)} %broadcast_in_dim.7), channel_id=1, replica_groups=mesh['req'=128,'tp'=4] {'tp'}, dimensions={0} | all-to-all | bytes 2097152 | tf_op jit(solution)/shard_map/all_to_all | solution.py:15
  52.4 1.9 %fusion.6 = bf16[512,768]{1,0:T(8,128)(2,1)} fusion(bf16[512,1024]{0,1:T(8,128)(2,1)S(1)} %bitcast.26, bf16[1024,256]{1,0:T(8,128)(2,1)S(1)} %copy-done.1, bf16[1024,256]{1,0:T(8,128)(2,1)S(1)} %copy-done.2, bf16[1024,256]{1,0:T(8,128)(2,1)S(1)} %copy-done.3), kind=kOutput, calls=%fused_computation.8 | convolution fusion | flops 810418176 | bytes 3407872 | tf_op jit(solution)/shard_map/dot_general | solution.py:136
  54.3 7.8 %shard_map.109 = bf16[2,256,256]{2,1,0:T(8,128)(2,1)} custom-call(s32[2]{0:T(128)} %lens_ref.1, bf16[2,256,768]{2,1,0:T(8,128)(2,1)} %bitcast.20, bf16[2,256,768]{2,1,0:T(8,128)(2,1)} %bitcast.21, bf16[2,256,768]{2,1,0:T(8,128)(2,1)} %bitcast.22, bf16[2,1024,256]{2,1,0:T(8,128)(2,1)} %kc_ref.1, bf16[2,1024,256]{2,1,0:T(8,128)(2,1)} %vc_ref.1), custom_call_target="tpu_custom_call" | custom-call | tf_op jit(solution)/shard_map/pallas_call | solution.py:74
  62.1 1.4 %convolution_convert_fusion = bf16[512,1024]{1,0:T(8,128)(2,1)S(1)} fusion(bf16[512,256]{1,0:T(8,128)(2,1)} %bitcast.25, bf16[256,1024]{1,0:T(8,128)(2,1)S(1)} %copy-done), kind=kOutput, calls=%fused_computation.7 | convolution fusion | flops 268959744 | bytes 1835008 | tf_op jit(solution)/shard_map/dot_general | solution.py:142
  63.5 14.5 %all_to_all.27 = bf16[4,512,256]{2,1,0:T(8,128)(2,1)S(1)} all-to-all(bf16[4,512,256]{2,1,0:T(8,128)(2,1)S(1)} %bitcast.24), channel_id=1, replica_groups=mesh['req'=128,'tp'=4] {'tp'}, dimensions={0} | all-to-all | bytes 2097152 | tf_op jit(solution)/shard_map/all_to_all | solution.py:23
  78.1 0.1 convert_reduce_fusion
  78.2 0.1 reduce_sum.39
  78.4 0.4 fusion.11
  79.0 0.6 broadcast_in_dim.8
  79.6 3.3 %all-to-all-start.3 = ((f32[4,2,512]{2,1,0:T(2,128)}), f32[4,2,512]{2,1,0:T(2,128)S(1)}, u32[]{:S(2)}, u32[]{:S(2)}) async-start(f32[4,2,512]{2,1,0:T(2,128)} %broadcast_in_dim.8), calls=%async_computation.3 | async-start | bytes 32768 | tf_op jit(solution)/shard_map/all_to_all | solution.py:30
  82.9 0.8 dynamic_slice.6
  83.7 0.8 dynamic_slice.7
  84.4 2.6 %all-to-all-done.3 = f32[4,2,512]{2,1,0:T(2,128)S(1)} async-done(((f32[4,2,512]{2,1,0:T(2,128)}), f32[4,2,512]{2,1,0:T(2,128)S(1)}, u32[]{:S(2)}, u32[]{:S(2)}) %all-to-all-start.3) | async-done | bytes 16416 | tf_op jit(solution)/shard_map/all_to_all | solution.py:30
  87.4 0.4 add_convert_fusion
  87.7 25.7 %all_to_all.28 = bf16[128,4,256]{2,1,0:T(4,128)(2,1)S(1)} all-to-all(bf16[128,4,256]{2,1,0:T(4,128)(2,1)S(1)} %add_convert_fusion), channel_id=1, replica_groups=mesh['req'=128,'tp'=4] {'req'}, dimensions={0} | all-to-all | bytes 524288 | tf_op jit(solution)/shard_map/all_to_all | solution.py:182
  113.4 0.3 convolution_convert_fusion.1
  113.7 0.2 copy.55
  113.9 0.8 reshape.80
  (19 shorter events, 0.7 us)
Async XLA Ops:
  0.0 62.1 %copy-start = (bf16[256,1024]{1,0:T(8,128)(2,1)S(1)}, bf16[256,1024]{1,0:T(8,128)(2,1)}, u32[]{:S(2)}) copy-start(bf16[256,1024]{1,0:T(8,128)(2,1)} %param.17) | copy-start | bytes 1572868
  35.1 17.2 %copy-start.1 = (bf16[1024,256]{1,0:T(8,128)(2,1)S(1)}, bf16[1024,256]{1,0:T(8,128)(2,1)}, u32[]{:S(2)}) copy-start(bf16[1024,256]{1,0:T(8,128)(2,1)} %param.16) | copy-start | bytes 1572868
  35.1 17.2 %copy-start.2 = (bf16[1024,256]{1,0:T(8,128)(2,1)S(1)}, bf16[1024,256]{1,0:T(8,128)(2,1)}, u32[]{:S(2)}) copy-start(bf16[1024,256]{1,0:T(8,128)(2,1)} %param.15) | copy-start | bytes 1572868
  35.1 17.2 %copy-start.3 = (bf16[1024,256]{1,0:T(8,128)(2,1)S(1)}, bf16[1024,256]{1,0:T(8,128)(2,1)}, u32[]{:S(2)}) copy-start(bf16[1024,256]{1,0:T(8,128)(2,1)} %param.14) | copy-start | bytes 1572868
  79.6 7.4 %all-to-all-start.3 = ((f32[4,2,512]{2,1,0:T(2,128)}), f32[4,2,512]{2,1,0:T(2,128)S(1)}, u32[]{:S(2)}, u32[]{:S(2)}) async-start(f32[4,2,512]{2,1,0:T(2,128)} %broadcast_in_dim.8), calls=%async_computation.3 | async-start | bytes 32768 | tf_op jit(solution)/shard_map/all_to_all | solution.py:30
